TPU v7x, 1024 devices: a whole 8x8x8 slice. The times are simulated.
1024 devices in a mesh: seq: 64 (over x, z_lo, core), clip: 16 (over y, z_hi).
Axes of the slice: x: 8, y: 8, z: 8 (z_hi: 2, z_lo: 4; z = z_hi * 4 + z_lo), core: 2. Of those that a mesh axis runs over, the one named last changes fastest.
Arguments:
- frames_in: bfloat16 [16, 64, 128, 768], P('clip', 'seq'), may hold values from -6 to 6
- norm_gains: float32 [2, 768], replicated, may hold values from 0.5 to 1.5
- space_proj: bfloat16 [768, 2304], replicated, may hold values from -0.21875 to 0.21875
- space_out: bfloat16 [768, 768], replicated, may hold values from -0.21875 to 0.21875
- time_proj: bfloat16 [768, 2304], replicated, may hold values from -0.21875 to 0.21875
- time_out: bfloat16 [768, 768], replicated, may hold values from -0.21875 to 0.21875
- qk_gains: float32 [4, 768], replicated, may hold values from 1 to 2.5
Outputs:
- block_out: bfloat16 [16, 64, 128, 768], P('clip', 'seq')
- clip_embed: float32 [16, 768], P('clip')
- similarity: float32 [16, 16], P('clip')
All inputs are finite; a program needn't handle non-finite values.
Results may differ from a plain program's by a relative error of at most 0.02.
Values may be sent and summed in bfloat16 or wider, within the bound.
No kernel may reach another device: no remote copies, remote signals or barrier semaphores. Data moves between devices by JAX's collectives and lax.ppermute only.
A program may use at most 32 MiB of HBM per device.

v0:
```python
import math

import jax
import jax.numpy as jnp
from jax import lax
from jax.sharding import PartitionSpec as P

D = 768
HEADS = 12


def from_everyone(array, axis):
    copies = jnp.broadcast_to(array, (lax.axis_size(axis), *array.shape))
    return lax.all_to_all(copies, axis, split_axis=0, concat_axis=0, tiled=True)


def over_copies(array, axis):
    return from_everyone(array, axis).sum(axis=0)


def laid_out(pieces, dim):
    pieces = jnp.moveaxis(pieces, 0, dim)
    dims = pieces.shape
    return pieces.reshape(*dims[:dim], dims[dim] * dims[dim + 1], *dims[dim + 2 :])


def collect(array, axis, dim):
    return laid_out(from_everyone(array, axis), dim)


def layer_norm(values, gains_row):
    widened = values.astype(jnp.float32)
    average = jnp.mean(widened, axis=-1, keepdims=True)
    centred = widened - average
    spread = jnp.mean(centred * centred, axis=-1, keepdims=True)
    return (centred * lax.rsqrt(spread + 1e-05) * gains_row).astype(jnp.bfloat16)


def head_norm(values, gains_row):
    inverse = lax.rsqrt(jnp.mean(values * values, axis=-1, keepdims=True) + 1e-06)
    return (values * inverse * gains_row.reshape(HEADS, -1)).astype(jnp.bfloat16)


def project(normed, proj):
    channels = normed.shape[-1]
    leading = normed.shape[:-1]
    projected = jnp.dot(normed.reshape(-1, channels), proj, preferred_element_type=jnp.float32)
    return projected.astype(jnp.bfloat16).reshape(leading + (proj.shape[1],))


def attention(projected, out_weight, gain_query, gain_key):
    channels = out_weight.shape[0]
    leading = projected.shape[:-1]
    head_size = channels // HEADS
    queries = projected[..., :channels].astype(jnp.float32).reshape(leading + (HEADS, head_size))
    key_part = (
        projected[..., channels : 2 * channels]
        .astype(jnp.float32)
        .reshape(leading + (HEADS, head_size))
    )
    value_part = projected[..., 2 * channels :].reshape(leading + (HEADS, head_size))
    query_n = head_norm(queries, gain_query)
    key_n = head_norm(key_part, gain_key)
    scores = jnp.einsum("...lhe,...mhe->...hlm", query_n, key_n, preferred_element_type=jnp.float32)
    scores = scores * (1.0 / math.sqrt(head_size))
    raised = jnp.exp(scores)
    attn_weights = (raised / jnp.sum(raised, axis=-1, keepdims=True)).astype(jnp.bfloat16)
    context = jnp.einsum(
        "...hlm,...mhe->...lhe", attn_weights, value_part, preferred_element_type=jnp.float32
    )
    context = context.astype(jnp.bfloat16).reshape(-1, channels)
    branch = jnp.dot(context, out_weight, preferred_element_type=jnp.float32)
    return branch.reshape(leading + (channels,))


def on_device(frames_in, norm_gains, space_proj, space_out, time_proj, time_out, qk_gains):
    clips_here, frames_here, patch_count, channels = frames_in.shape
    groups = lax.axis_size("seq")
    per_group = patch_count // groups
    spatial_in = layer_norm(frames_in, norm_gains[0])
    branch = attention(project(spatial_in, space_proj), space_out, qk_gains[0], qk_gains[1])
    middle = (frames_in.astype(jnp.float32) + branch).astype(jnp.bfloat16)
    temporal_in = layer_norm(middle, norm_gains[1])
    outgoing = temporal_in.reshape(clips_here, groups, per_group, frames_here, channels)
    arrived = attention(
        project(
            lax.all_to_all(outgoing, "seq", split_axis=1, concat_axis=3, tiled=True), time_proj
        ),
        time_out,
        qk_gains[2],
        qk_gains[3],
    ).astype(jnp.bfloat16)
    returned = lax.all_to_all(arrived, "seq", split_axis=3, concat_axis=1, tiled=True)
    returned = returned.reshape(clips_here, frames_here, patch_count, channels)
    block_out = (middle.astype(jnp.float32) + returned.astype(jnp.float32)).astype(jnp.bfloat16)
    local_sum = jnp.sum(block_out.astype(jnp.float32), axis=(1, 2))
    pooled_total = over_copies(local_sum, "seq")
    pooled = pooled_total / (frames_here * patch_count * groups)
    clip_embed = pooled * lax.rsqrt(jnp.mean(pooled * pooled, axis=-1, keepdims=True) + 1e-06)
    all_embeds = collect(clip_embed, "clip", 0)
    similarity = (
        jnp.dot(
            clip_embed,
            all_embeds.T,
            precision=lax.Precision.HIGHEST,
            preferred_element_type=jnp.float32,
        )
        / D
    )
    return (block_out, clip_embed, similarity)


def solution(mesh):
    return jax.shard_map(
        on_device,
        mesh=mesh,
        in_specs=(P("clip", "seq", None, None), P(), P(), P(), P(), P(), P()),
        out_specs=(P("clip", "seq", None, None), P("clip", None), P("clip", None)),
        check_vma=False,
    )
```

profile of v0, /device:TPU:1, one launch (start us, length us, event | category | flops | bytes accessed | tf_op | source)
XLA Modules:
  0.0 163.7 jit_solution(11420251240459951732)
XLA Ops:
  0.6 0.0 copy-start
  0.6 1.5 slice_reduce_fusion.2
  2.1 1.0 convert_reduce_fusion
  3.2 1.1 fusion.18
  4.3 1.6 fusion
  5.9 0.9 fusion.35
  6.9 1.0 slice_convert_fusion.2
  7.8 1.9 %copy.61 = f32[1,1,128,768]{2,3,1,0:T(8,128)} copy(f32[1,1,128,768]{3,2,1,0:T(8,128)} %get-tuple-element.16) | data formatting | bytes 786432 | tf_op jit(solution)/shard_map/mul | solution.py:40
  9.7 1.9 %copy.63 = f32[1,1,128,768]{2,3,1,0:T(8,128)} copy(f32[1,1,128,768]{3,2,1,0:T(8,128)} %get-tuple-element.17) | data formatting | bytes 786432 | tf_op jit(solution)/shard_map/mul | solution.py:40
  11.7 1.6 reduce_sum.119
  13.3 1.6 reduce_sum.120
  14.9 1.9 %copy.60 = f32[1,1,128,768]{2,3,1,0:T(8,128)} copy(f32[1,1,128,768]{3,2,1,0:T(8,128)} %get-tuple-element.19) | data formatting | bytes 786432 | tf_op jit(solution)/shard_map/convert_element_type | solution.py:55
  16.8 1.9 %copy.62 = f32[1,1,128,768]{2,3,1,0:T(8,128)} copy(f32[1,1,128,768]{3,2,1,0:T(8,128)} %get-tuple-element.18) | data formatting | bytes 786432 | tf_op jit(solution)/shard_map/convert_element_type | solution.py:58
  18.7 1.5 slice_reduce_fusion.1
  20.2 0.1 mul.263
  20.3 0.8 mul.270
  21.1 1.7 %copy.59 = bf16[1,1,128,768]{2,3,1,0:T(8,128)(2,1)} copy(bf16[1,1,128,768]{3,2,1,0:T(8,128)(2,1)} %get-tuple-element.20) | data formatting | bytes 393216 | tf_op jit(solution)/shard_map/slice | solution.py:61
  22.8 0.7 add_rsqrt_fusion.2
  23.5 2.6 %fusion.2 = f32[12,128,128]{1,2,0:T(8,128)} fusion(f32[128,12,64]{0,2,1:T(8,128)} %bitcast.88, f32[128,12,64]{0,2,1:T(8,128)} %bitcast.89, f32[12,64]{1,0:T(8,128)S(1)} %mul.270, f32[128,12]{0,1:T(8,128)S(1)} %get-tuple-element.23, f32[12,64]{1,0:T(8,128)S(1)} %mul.263, f32[128,12]{0,1:T(8,128)S(1)} %get-tuple-element.24), kind=kOutput, calls=%fused_computation.6 | convolution fusion | flops 25952256 | bytes 1591296 | tf_op jit(solution)/shard_map/...lhe,...mhe->...hlm/dot_general | solution.py:64
  26.1 2.4 %convolution_convert_fusion.3 = bf16[12,64,128]{2,1,0:T(8,128)(2,1)} fusion(bf16[128,12,64]{0,2,1:T(8,128)(2,1)} %bitcast.95, f32[12,128,128]{1,2,0:T(8,128)} %fusion.2), kind=kOutput, calls=%fused_computation.15 | convolution fusion | flops 25659008 | bytes 1179648 | tf_op jit(solution)/shard_map/...hlm,...mhe->...lhe/dot_general | solution.py:68
  28.5 1.8 %fusion.49 = (f32[128]{0:T(128)S(1)}, f32[1,1,128,768]{3,2,1,0:T(8,128)S(1)}) fusion(bf16[128,768]{0,1:T(8,128)(2,1)} %bitcast.94, bf16[768,768]{1,0:T(8,128)(2,1)} %param.10, bf16[1,1,128,768]{3,2,1,0:T(8,128)(2,1)} %param.7), kind=kOutput, calls=%fused_computation.80 | convolution fusion | flops 151486336 | bytes 1966592 | tf_op jit(solution)/shard_map/dot_general | solution.py:72
  30.3 0.2 multiply_reduce_fusion
  30.5 0.5 copy-done.1
  31.1 0.8 multiply_convert_fusion.2
  31.9 1.7 %reshape.352 = bf16[1,64,2,1,768]{4,2,1,3,0:T(2,128)(2,1)} reshape(bf16[1,1,128,768]{3,2,1,0:T(8,128)(2,1)} %multiply_convert_fusion.2) | data formatting | bytes 393216 | tf_op jit(solution)/shard_map/reshape | solution.py:84
  33.5 18.9 %all-to-all-start = ((bf16[1,64,2,1,768]{4,2,3,0,1:T(2,128)(2,1)}), bf16[1,64,2,1,768]{4,2,3,0,1:T(2,128)(2,1)}, u32[]{:S(2)}, u32[]{:S(2)}) async-start(bf16[1,64,2,1,768]{4,2,3,0,1:T(2,128)(2,1)} %bitcast.91), calls=%async_computation | async-start | bytes 393216 | tf_op jit(solution)/shard_map/all_to_all | solution.py:87
  52.5 0.0 copy-done.5
  52.5 0.1 mul.285
  52.5 0.8 mul.292
  53.3 10.8 %all-to-all-done = bf16[1,64,2,1,768]{4,2,3,0,1:T(2,128)(2,1)} async-done(((bf16[1,64,2,1,768]{4,2,3,0,1:T(2,128)(2,1)}), bf16[1,64,2,1,768]{4,2,3,0,1:T(2,128)(2,1)}, u32[]{:S(2)}, u32[]{:S(2)}) %all-to-all-start) | async-done | bytes 196640 | tf_op jit(solution)/shard_map/all_to_all | solution.py:87
  64.1 0.9 copy.66
  65.1 2.7 %convolution_convert_fusion = bf16[128,2304]{1,0:T(8,128)(2,1)S(1)} fusion(bf16[128,768]{1,0:T(8,128)(2,1)S(1)} %bitcast.90, bf16[768,2304]{1,0:T(8,128)(2,1)} %param.11), kind=kOutput, calls=%fused_computation | convolution fusion | flops 453279744 | bytes 4325376 | tf_op jit(solution)/shard_map/dot_general | solution.py:47
  67.7 1.0 slice_convert_fusion.1
  68.7 1.0 fusion.37
  69.7 2.2 %reshape.356 = f32[2,64,12,64]{3,2,1,0:T(8,128)} reshape(f32[1,1,2,64,768]{4,3,2,1,0:T(8,128)} %get-tuple-element.13) | data formatting | bytes 786432 | tf_op jit(solution)/shard_map/reshape | solution.py:55
  71.9 2.3 %mul.282 = f32[2,64,12,64]{3,2,1,0:T(8,128)} reshape(f32[1,1,2,64,768]{4,3,2,1,0:T(8,128)} %get-tuple-element.11) | data formatting | bytes 786432 | tf_op jit(solution)/shard_map/mul | solution.py:40
  74.2 2.2 %reduce_sum.124 = f32[2,64,12]{2,1,0:T(8,128)} reduce(f32[2,64,12,64]{3,2,1,0:T(8,128)} %mul.282, f32[]{:T(128)} %constant.28.clone.1), dimensions={3}, to_apply=%region_7.0 | reduce | flops 96768 | bytes 399364 | tf_op jit(solution)/shard_map/reduce_sum | solution.py:40
  76.4 1.5 add_rsqrt_fusion.1
  77.8 2.3 %reshape.357 = f32[2,64,12,64]{3,2,1,0:T(8,128)} reshape(f32[1,1,2,64,768]{4,3,2,1,0:T(8,128)} %get-tuple-element.14) | data formatting | bytes 786432 | tf_op jit(solution)/shard_map/reshape | solution.py:59
  80.1 2.2 %mul.289 = f32[2,64,12,64]{3,2,1,0:T(8,128)} reshape(f32[1,1,2,64,768]{4,3,2,1,0:T(8,128)} %get-tuple-element.12) | data formatting | bytes 786432 | tf_op jit(solution)/shard_map/mul | solution.py:40
  82.3 2.2 %reduce_sum.125 = f32[2,64,12]{2,1,0:T(8,128)} reduce(f32[2,64,12,64]{3,2,1,0:T(8,128)} %mul.289, f32[]{:T(128)} %constant.28.clone.1), dimensions={3}, to_apply=%region_8.0 | reduce | flops 96768 | bytes 399364 | tf_op jit(solution)/shard_map/reduce_sum | solution.py:40
  84.5 1.5 add_rsqrt_fusion
  86.0 1.9 %copy.67 = bf16[1,1,2,64,768]{3,4,2,1,0:T(8,128)(2,1)} copy(bf16[1,1,2,64,768]{4,3,2,1,0:T(8,128)(2,1)} %get-tuple-element.15) | data formatting | bytes 393216 | tf_op jit(solution)/shard_map/slice | solution.py:61
  87.9 1.7 %multiply_convert_fusion.1 = bf16[2,64,12,64]{3,2,1,0:T(8,128)(2,1)S(1)} fusion(f32[2,64,12,64]{3,2,1,0:T(8,128)} %reshape.356, f32[12,64]{1,0:T(8,128)S(1)} %mul.285, f32[2,64,12]{2,1,0:T(8,128)} %add_rsqrt_fusion.1), kind=kLoop, calls=%fused_computation.21 | loop fusion | flops 294912 | bytes 599040 | tf_op jit(solution)/shard_map/convert_element_type | solution.py:41
  89.5 0.0 copy-done.2
  89.5 0.0 copy-done.3
  89.5 0.3 multiply_convert_fusion
  89.9 1.2 fusion.1
  91.1 2.5 %convolution_convert_fusion.2 = bf16[2,12,64,64]{3,2,1,0:T(8,128)(2,1)} fusion(bf16[2,64,12,64]{1,3,2,0:T(8,128)(2,1)} %bitcast.93, f32[2,12,64,64]{2,3,1,0:T(8,128)} %fusion.1), kind=kOutput, calls=%fused_computation.7 | convolution fusion | flops 12879423 | bytes 786432 | tf_op jit(solution)/shard_map/...hlm,...mhe->...lhe/dot_general | solution.py:68
  93.6 1.7 %fusion.11 = bf16[1,1,2,64,768]{4,3,2,1,0:T(8,128)(2,1)S(1)} fusion(bf16[2,64,768]{1,2,0:T(8,128)(2,1)} %bitcast.92, bf16[768,768]{1,0:T(8,128)(2,1)} %param.12), kind=kOutput, calls=%fused_computation.16 | convolution fusion | flops 151093248 | bytes 1572864 | tf_op jit(solution)/shard_map/dot_general | solution.py:72
  95.4 0.2 copy.72
  95.6 15.9 %all_to_all.34 = bf16[1,1,2,64,768]{4,2,1,0,3:T(2,128)(2,1)S(1)} all-to-all(bf16[1,1,2,64,768]{4,2,1,0,3:T(2,128)(2,1)S(1)} %copy.72), channel_id=1, replica_groups=mesh['seq'=64,'clip'=16] {'seq'}, dimensions={3} | all-to-all | bytes 393216 | tf_op jit(solution)/shard_map/all_to_all | solution.py:93
  111.5 0.9 convert_bitcast_fusion
  112.4 2.0 %reshape.359 = f32[1,1,128,768]{3,2,1,0:T(8,128)} reshape(f32[1,64,1,2,1,768]{5,3,1,4,2,0:T(2,128)} %convert_bitcast_fusion) | data formatting | bytes 786432 | tf_op jit(solution)/shard_map/convert_element_type | solution.py:95
  114.4 1.8 %convert_reduce_fusion.1 = (f32[768]{0:T(1024)S(1)}, bf16[1,1,128,768]{3,2,1,0:T(8,128)(2,1)}) fusion(f32[1,1,128,768]{3,2,1,0:T(8,128)} %copy-done.1, f32[1,1,128,768]{3,2,1,0:T(8,128)} %reshape.359), kind=kLoop, calls=%fused_computation.34 | loop fusion | flops 392448 | bytes 986112 | tf_op jit(solution)/shard_map/reduce_sum | solution.py:96
  116.3 0.1 broadcast_in_dim.4
  116.4 16.2 %all_to_all.35 = f32[64,1,768]{2,1,0:T(1,128)} all-to-all(f32[64,1,768]{2,1,0:T(1,128)S(1)} %broadcast_in_dim.4), channel_id=1, replica_groups=mesh['seq'=64,'clip'=16] {'seq'}, dimensions={0} | all-to-all | bytes 393216 | tf_op jit(solution)/shard_map/all_to_all | solution.py:14
  132.5 1.1 reduce_sum.128
  133.6 0.6 multiply_reduce_fusion.1
  134.9 0.6 broadcast_in_dim.5
  135.5 14.9 %all-to-all-start.3 = ((f32[16,1,768]{2,1,0:T(1,128)}), f32[16,1,768]{2,1,0:T(1,128)}, u32[]{:S(2)}, u32[]{:S(2)}) async-start(f32[16,1,768]{2,1,0:T(1,128)} %broadcast_in_dim.5), calls=%async_computation.3 | async-start | bytes 98304 | tf_op jit(solution)/shard_map/all_to_all | solution.py:14
  150.5 0.6 mul.301
  151.1 11.1 %all-to-all-done.3 = f32[16,1,768]{2,1,0:T(1,128)} async-done(((f32[16,1,768]{2,1,0:T(1,128)}), f32[16,1,768]{2,1,0:T(1,128)}, u32[]{:S(2)}, u32[]{:S(2)}) %all-to-all-start.3) | async-done | bytes 49184 | tf_op jit(solution)/shard_map/all_to_all | solution.py:14
  162.2 1.5 fusion.15
  (13 shorter events, 0.0 us)
Async XLA Ops:
  0.6 3.7 %copy-start = (bf16[768,2304]{1,0:T(8,128)(2,1)S(1)}, bf16[768,2304]{1,0:T(8,128)(2,1)}, u32[]{:S(2)}) copy-start(bf16[768,2304]{1,0:T(8,128)(2,1)} %param.9) | copy-start | bytes 10616836
  28.5 2.5 %copy-start.4 = (f32[768]{0:T(1024)S(1)}, f32[768]{0:T(1024)}, u32[]{:S(2)}) copy-start(f32[768]{0:T(1024)} %get-tuple-element.7) | copy-start | bytes 9220
  30.3 0.8 copy-start.1
  30.3 22.1 %copy-start.5 = (f32[768]{0:T(1024)S(1)}, f32[768]{0:T(1024)}, u32[]{:S(2)}) copy-start(f32[768]{0:T(1024)} %get-tuple-element.3) | copy-start | bytes 9220
  33.5 30.6 %all-to-all-start = ((bf16[1,64,2,1,768]{4,2,3,0,1:T(2,128)(2,1)}), bf16[1,64,2,1,768]{4,2,3,0,1:T(2,128)(2,1)}, u32[]{:S(2)}, u32[]{:S(2)}) async-start(bf16[1,64,2,1,768]{4,2,3,0,1:T(2,128)(2,1)} %bitcast.91), calls=%async_computation | async-start | bytes 393216 | tf_op jit(solution)/shard_map/all_to_all | solution.py:87
  87.8 1.7 %copy-start.2 = (f32[2,64,12,64]{3,2,1,0:T(8,128)S(1)}, f32[2,64,12,64]{3,2,1,0:T(8,128)}, u32[]{:S(2)}) copy-start(f32[2,64,12,64]{3,2,1,0:T(8,128)} %reshape.357) | copy-start | bytes 1179652
  87.8 1.7 %copy-start.3 = (f32[2,64,12]{2,1,0:T(8,128)S(1)}, f32[2,64,12]{2,1,0:T(8,128)}, u32[]{:S(2)}) copy-start(f32[2,64,12]{2,1,0:T(8,128)} %add_rsqrt_fusion) | copy-start | bytes 18436
  135.5 26.7 %all-to-all-start.3 = ((f32[16,1,768]{2,1,0:T(1,128)}), f32[16,1,768]{2,1,0:T(1,128)}, u32[]{:S(2)}, u32[]{:S(2)}) async-start(f32[16,1,768]{2,1,0:T(1,128)} %broadcast_in_dim.5), calls=%async_computation.3 | async-start | bytes 98304 | tf_op jit(solution)/shard_map/all_to_all | solution.py:14
where the time goes:
time: 165 us; the launch traced here: 164 us
  starting transfers between devices  33.8 us (20%)
  blocking collectives  32.1 us (19%)
  local copies, waits for them, and re-layouts  31.6 us (19%)
  other arithmetic  24.7 us (15%)
  waiting for transfers between devices  22 us (13%)
  matrix products  18 us (11%)
    all_to_all x1, starting transfers between devices, on_device(): lax.all_to_all(outgoing, 'seq', split_axis=1, concat_axis=3, tiled=True)  18.9 us
    all_to_all x1, blocking collectives, from_everyone(): return lax.all_to_all(copies, axis, split_axis=0, concat_axis=0, tiled=True)  16.2 us
    all_to_all x1, blocking collectives, on_device(): lax.all_to_all(arrived, 'seq', split_axis=3, concat_axis=1, tiled=True)  15.9 us
    all_to_all x1, starting transfers between devices, from_everyone(): return lax.all_to_all(copies, axis, split_axis=0, concat_axis=0, tiled=True)  14.9 us
    all_to_all x1, waiting for transfers between devices, from_everyone(): return lax.all_to_all(copies, axis, split_axis=0, concat_axis=0, tiled=True)  11.1 us
    all_to_all x1, waiting for transfers between devices, on_device(): lax.all_to_all(outgoing, 'seq', split_axis=1, concat_axis=3, tiled=True)  10.8 us
    mul x4, local copies, waits for them, and re-layouts, head_norm(): values * values  8.34 us
    reduce_sum x4, other arithmetic, head_norm(): jnp.mean(values * values, axis=-1, keepdims=True) + 1e-06  7.62 us
  transfers between devices with their start and end apart: 2, of which 2 were waited for; matrix products, arithmetic and copies ran while one was open for 1% of the time, Pallas kernels for 0%

commit v1 on v0

--- a/solution.py
+++ b/solution.py
@@ -94,10 +94,10 @@
     returned = returned.reshape(clips_here, frames_here, patch_count, channels)
     block_out = (middle.astype(jnp.float32) + returned.astype(jnp.float32)).astype(jnp.bfloat16)
     local_sum = jnp.sum(block_out.astype(jnp.float32), axis=(1, 2))
-    pooled_total = over_copies(local_sum, "seq")
+    pooled_total = lax.psum(local_sum, "seq")
     pooled = pooled_total / (frames_here * patch_count * groups)
     clip_embed = pooled * lax.rsqrt(jnp.mean(pooled * pooled, axis=-1, keepdims=True) + 1e-06)
-    all_embeds = collect(clip_embed, "clip", 0)
+    all_embeds = lax.all_gather(clip_embed, "clip", axis=0, tiled=True)
     similarity = (
         jnp.dot(
             clip_embed,

time: 165 us -> 309 us (1.87)
  the two profiles are of different devices: /device:TPU:1 before, /device:TPU:16 now
where the time goes in v1:
time: 309 us; the launch traced here: 307 us
  blocking collectives  208 us (67%)
  local copies, waits for them, and re-layouts  30.3 us (10%)
  other arithmetic  23.6 us (8%)
  matrix products  17.2 us (6%)
  starting transfers between devices  16.2 us (5%)
  waiting for transfers between devices  10.5 us (3%)
    psum x1, blocking collectives, on_device(): pooled_total = lax.psum(local_sum, 'seq')  135 us
    all_gather x1, blocking collectives, on_device(): all_embeds = lax.all_gather(clip_embed, 'clip', axis=0, tiled=True)  56.7 us
    all_to_all x1, starting transfers between devices, on_device(): lax.all_to_all(outgoing, 'seq', split_axis=1, concat_axis=3, tiled=True)  16.2 us
    all_to_all x1, blocking collectives, on_device(): lax.all_to_all(arrived, 'seq', split_axis=3, concat_axis=1, tiled=True)  16.1 us
    all_to_all x1, waiting for transfers between devices, on_device(): lax.all_to_all(outgoing, 'seq', split_axis=1, concat_axis=3, tiled=True)  10.5 us
    mul x4, local copies, waits for them, and re-layouts, head_norm(): values * values  8.34 us
    reduce_sum x4, other arithmetic, head_norm(): jnp.mean(values * values, axis=-1, keepdims=True) + 1e-06  7.62 us
  transfers between devices with their start and end apart: 1, of which 1 were waited for; matrix products, arithmetic and copies ran while one was open for 0% of the time, Pallas kernels for 0%

profile of v1, /device:TPU:16, one launch (start us, length us, event | category | flops | bytes accessed | tf_op | source)
XLA Modules:
  0.0 307.4 jit_solution(6234011822543015140)
XLA Ops:
  0.6 0.0 copy-start
  0.6 1.5 slice_reduce_fusion.2
  2.1 1.0 convert_reduce_fusion
  3.2 1.1 fusion.18
  4.3 0.0 copy-done
  4.3 1.6 fusion
  5.9 0.9 fusion.35
  6.9 1.0 slice_convert_fusion.2
  7.8 1.9 copy.33
  9.7 1.9 copy.35
  11.7 1.6 reduce_sum.112
  13.3 1.6 reduce_sum.113
  14.9 1.9 copy.32
  16.8 1.9 copy.34
  18.7 1.5 slice_reduce_fusion.1
  20.2 0.1 mul.243
  20.3 0.8 mul.250
  21.1 1.7 copy.31
  22.8 0.7 add_rsqrt_fusion.2
  23.5 2.6 fusion.2
  26.1 2.4 convolution_convert_fusion.3
  28.5 1.8 fusion.50
  30.3 0.0 copy-start.1
  30.3 0.0 copy-start.5
  30.3 0.2 multiply_reduce_fusion
  30.5 0.5 copy-done.1
  31.1 0.0 copy-done.4
  31.1 0.8 multiply_convert_fusion.2
  31.9 1.7 reshape.327
  33.5 16.2 %all-to-all-start = ((bf16[1,64,2,1,768]{4,2,3,0,1:T(2,128)(2,1)}), bf16[1,64,2,1,768]{4,2,3,0,1:T(2,128)(2,1)}, u32[]{:S(2)}, u32[]{:S(2)}) async-start(bf16[1,64,2,1,768]{4,2,3,0,1:T(2,128)(2,1)} %bitcast.95), calls=%async_computation | async-start | bytes 393216 | tf_op jit(solution)/shard_map/all_to_all | solution.py:87
  49.7 0.0 copy-done.5
  49.7 0.1 mul.265
  49.8 0.8 mul.272
  50.5 10.5 %all-to-all-done = bf16[1,64,2,1,768]{4,2,3,0,1:T(2,128)(2,1)} async-done(((bf16[1,64,2,1,768]{4,2,3,0,1:T(2,128)(2,1)}), bf16[1,64,2,1,768]{4,2,3,0,1:T(2,128)(2,1)}, u32[]{:S(2)}, u32[]{:S(2)}) %all-to-all-start) | async-done | bytes 196640 | tf_op jit(solution)/shard_map/all_to_all | solution.py:87
  61.0 0.9 copy.38
  62.0 2.7 convolution_convert_fusion
  64.6 1.0 slice_convert_fusion.1
  65.6 1.0 fusion.37
  66.6 2.2 reshape.331
  68.8 2.3 mul.262
  71.1 2.2 reduce_sum.117
  73.3 1.5 add_rsqrt_fusion.1
  74.7 2.3 reshape.332
  77.0 2.2 mul.269
  79.2 2.2 reduce_sum.118
  81.4 1.5 add_rsqrt_fusion
  82.9 1.9 copy.39
  84.8 1.7 multiply_convert_fusion.1
  86.4 0.0 copy-done.2
  86.4 0.0 copy-done.3
  86.5 0.3 multiply_convert_fusion
  86.8 1.2 fusion.1
  88.0 2.5 convolution_convert_fusion.2
  90.5 1.7 fusion.11
  92.3 0.2 copy.44
  92.5 16.1 %all_to_all.24 = bf16[1,1,2,64,768]{4,2,1,0,3:T(2,128)(2,1)S(1)} all-to-all(bf16[1,1,2,64,768]{4,2,1,0,3:T(2,128)(2,1)S(1)} %copy.44), channel_id=1, replica_groups=mesh['seq'=64,'clip'=16] {'seq'}, dimensions={3} | all-to-all | bytes 393216 | tf_op jit(solution)/shard_map/all_to_all | solution.py:93
  108.6 0.9 convert_bitcast_fusion
  109.4 2.0 reshape.334
  111.4 1.8 convert_reduce_fusion.1
  113.3 135.4 %psum.7 = f32[1,768]{1,0:T(1,128)S(1)} all-reduce(f32[1,768]{1,0:T(1,128)S(1)} %reduce_sum.121), channel_id=1, replica_groups=mesh['seq'=64,'clip'=16] {'seq'}, use_global_device_ids=true, to_apply=%region_11.0 | all-reduce | flops 768 | bytes 6144 | tf_op jit(solution)/shard_map/psum | solution.py:97
  248.7 0.6 multiply_reduce_fusion.1
  250.0 0.0 copy-start.6
  250.0 56.7 %all-gather = f32[16,1,768]{2,1,0:T(1,128)S(1)} all-gather(f32[1,1,768]{2,1,0:T(1,128)S(1)} %fusion.61), channel_id=1, replica_groups=mesh['seq'=64,'clip'=16] {'clip'}, dimensions={0}, use_global_device_ids=true | all-gather | bytes 52224 | tf_op jit(solution)/shard_map/all_gather | solution.py:100
  306.7 0.7 fusion.15
  (11 shorter events, 0.0 us)
Async XLA Ops:
  0.6 3.7 %copy-start = (bf16[768,2304]{1,0:T(8,128)(2,1)S(1)}, bf16[768,2304]{1,0:T(8,128)(2,1)}, u32[]{:S(2)}) copy-start(bf16[768,2304]{1,0:T(8,128)(2,1)} %param.9) | copy-start | bytes 10616836
  28.5 2.5 copy-start.4
  30.3 0.8 copy-start.1
  30.3 19.4 %copy-start.5 = (f32[768]{0:T(1024)S(1)}, f32[768]{0:T(1024)}, u32[]{:S(2)}) copy-start(f32[768]{0:T(1024)} %get-tuple-element.3) | copy-start | bytes 9220
  33.5 27.5 %all-to-all-start = ((bf16[1,64,2,1,768]{4,2,3,0,1:T(2,128)(2,1)}), bf16[1,64,2,1,768]{4,2,3,0,1:T(2,128)(2,1)}, u32[]{:S(2)}, u32[]{:S(2)}) async-start(bf16[1,64,2,1,768]{4,2,3,0,1:T(2,128)(2,1)} %bitcast.95), calls=%async_computation | async-start | bytes 393216 | tf_op jit(solution)/shard_map/all_to_all | solution.py:87
  84.8 1.7 copy-start.2
  84.8 1.7 copy-start.3
  250.0 57.4 %copy-start.6 = (f32[1,768]{1,0:T(1,128)}, f32[1,768]{1,0:T(1,128)S(1)}, u32[]{:S(2)}) copy-start(f32[1,768]{1,0:T(1,128)S(1)} %broadcast_multiply_fusion) | copy-start | bytes 9220

commit v2 on v0

--- a/solution.py
+++ b/solution.py
@@ -80,21 +80,24 @@
     spatial_in = layer_norm(frames_in, norm_gains[0])
     branch = attention(project(spatial_in, space_proj), space_out, qk_gains[0], qk_gains[1])
     middle = (frames_in.astype(jnp.float32) + branch).astype(jnp.bfloat16)
-    temporal_in = layer_norm(middle, norm_gains[1])
-    outgoing = temporal_in.reshape(clips_here, groups, per_group, frames_here, channels)
-    arrived = attention(
-        project(
-            lax.all_to_all(outgoing, "seq", split_axis=1, concat_axis=3, tiled=True), time_proj
-        ),
-        time_out,
-        qk_gains[2],
-        qk_gains[3],
+    outgoing = middle.reshape(clips_here, groups, per_group, frames_here, channels)
+    arrived = lax.all_to_all(outgoing, "seq", split_axis=1, concat_axis=3, tiled=True)
+    temporal_in = layer_norm(arrived, norm_gains[1])
+    branch_t = attention(
+        project(temporal_in, time_proj), time_out, qk_gains[2], qk_gains[3]
     ).astype(jnp.bfloat16)
-    returned = lax.all_to_all(arrived, "seq", split_axis=3, concat_axis=1, tiled=True)
-    returned = returned.reshape(clips_here, frames_here, patch_count, channels)
-    block_out = (middle.astype(jnp.float32) + returned.astype(jnp.float32)).astype(jnp.bfloat16)
-    local_sum = jnp.sum(block_out.astype(jnp.float32), axis=(1, 2))
-    pooled_total = over_copies(local_sum, "seq")
+    block_t = (arrived.astype(jnp.float32) + branch_t.astype(jnp.float32)).astype(jnp.bfloat16)
+    partial = jnp.sum(block_t.astype(jnp.float32), axis=(2, 3), keepdims=True)
+    high = partial.astype(jnp.bfloat16)
+    low = (partial - high.astype(jnp.float32)).astype(jnp.bfloat16)
+    spread_shape = (clips_here, 1, 1, block_t.shape[3], channels)
+    payload = jnp.concatenate(
+        [block_t, jnp.broadcast_to(high, spread_shape), jnp.broadcast_to(low, spread_shape)], axis=2
+    )
+    returned = lax.all_to_all(payload, "seq", split_axis=3, concat_axis=1, tiled=True)
+    block_out = returned[:, :, :per_group].reshape(clips_here, frames_here, patch_count, channels)
+    sums = returned[:, :, per_group:].astype(jnp.float32)
+    pooled_total = jnp.sum(sums, axis=(1, 2, 3))
     pooled = pooled_total / (frames_here * patch_count * groups)
     clip_embed = pooled * lax.rsqrt(jnp.mean(pooled * pooled, axis=-1, keepdims=True) + 1e-06)
     all_embeds = collect(clip_embed, "clip", 0)

time: 165 us -> 153 us (0.927)
  blocking collectives: 32.1 us -> 19.5 us
  waiting for transfers between devices: 22 us -> 18.5 us
  local copies, waits for them, and re-layouts: 31.6 us -> 34.9 us
    all_to_all x2 -> x1, blocking collectives: 32.1 us -> 19.5 us  [on_device(): lax.all_to_all(payload, 'seq', split_axis=3, concat_axis=1, tiled=True)]
    all_to_all x1, waiting for transfers between devices: 11.1 us -> 7.66 us  [from_everyone(): return lax.all_to_all(copies, axis, split_axis=0, concat_axis=0, tiled=True)]
    reduce_sum x2 -> x1, other arithmetic: 2.91 us -> 0.28 us  [on_device(): pooled_total = jnp.sum(sums, axis=(1, 2, 3))]
    convert_element_type x2 -> x0, local copies, waits for them, and re-layouts: 2.21 us -> none  [the longest x1 2 us: on_device(): returned.astype(jnp.float32)]
    slice x1 -> x2, local copies, waits for them, and re-layouts: 1.46 us -> 3.26 us  [the longest x1 1.8 us: on_device(): returned[:, :, :per_group]]
    reshape x1 -> x2, local copies, waits for them, and re-layouts: 1.68 us -> 3.36 us  [the longest x1 1.68 us: on_device(): returned[:, :, :per_group]]
  transfers between devices with their start and end apart: 2 -> 2, of which waited for: 2 -> 2; matrix products, arithmetic and copies ran while one was open for 1% -> 3% of each run, Pallas kernels for 0% -> 0%
where the time goes in v2:
time: 153 us; the launch traced here: 151 us
  local copies, waits for them, and re-layouts  34.9 us (23%)
  starting transfers between devices  33.8 us (22%)
  other arithmetic  24.6 us (16%)
  blocking collectives  19.5 us (13%)
  matrix products  18.6 us (12%)
  waiting for transfers between devices  18.5 us (12%)
    all_to_all x1, blocking collectives, on_device(): lax.all_to_all(payload, 'seq', split_axis=3, concat_axis=1, tiled=True)  19.5 us
    all_to_all x1, starting transfers between devices, on_device(): lax.all_to_all(outgoing, 'seq', split_axis=1, concat_axis=3, tiled=True)  18.9 us
    all_to_all x1, starting transfers between devices, from_everyone(): return lax.all_to_all(copies, axis, split_axis=0, concat_axis=0, tiled=True)  14.9 us
    all_to_all x1, waiting for transfers between devices, on_device(): lax.all_to_all(outgoing, 'seq', split_axis=1, concat_axis=3, tiled=True)  10.8 us
    mul x4, local copies, waits for them, and re-layouts, head_norm(): values * values  8.34 us
    all_to_all x1, waiting for transfers between devices, from_everyone(): return lax.all_to_all(copies, axis, split_axis=0, concat_axis=0, tiled=True)  7.66 us
    reduce_sum x4, other arithmetic, head_norm(): jnp.mean(values * values, axis=-1, keepdims=True) + 1e-06  7.62 us
    dot_general x2, matrix products, attention(): jnp.einsum('...hlm,...mhe->...lhe', attn_weights, value_part, preferred_e...  4.9 us
  transfers between devices with their start and end apart: 2, of which 2 were waited for; matrix products, arithmetic and copies ran while one was open for 3% of the time, Pallas kernels for 0%

profile of v2, /device:TPU:1, one launch (start us, length us, event | category | flops | bytes accessed | tf_op | source)
XLA Modules:
  0.0 151.4 jit_solution(3879561859350167522)
XLA Ops:
  0.6 0.0 copy-start
  0.6 1.5 slice_reduce_fusion.5
  2.1 1.0 convert_reduce_fusion
  3.2 1.1 fusion.23
  4.3 0.0 copy-done
  4.3 1.6 %fusion = bf16[1,1,128,2304]{3,2,1,0:T(8,128)(2,1)S(1)} fusion(bf16[768,2304]{1,0:T(8,128)(2,1)S(1)} %copy-done, bf16[1,1,128,768]{3,2,1,0:T(8,128)(2,1)} %param.7, f32[768]{0:T(1024)S(1)} %get-tuple-element.7, f32[128]{0:T(128)S(1)} %add_rsqrt_fusion.5, f32[128]{0:T(128)S(1)} %broadcast_multiply_fusion.2), kind=kOutput, calls=%fused_computation.2 | convolution fusion | flops 453771264 | bytes 4329472 | tf_op jit(solution)/shard_map/dot_general | solution.py:47
  5.9 0.9 fusion.45
  6.9 1.0 slice_convert_fusion.2
  7.8 1.9 %copy.33 = f32[1,1,128,768]{2,3,1,0:T(8,128)} copy(f32[1,1,128,768]{3,2,1,0:T(8,128)} %get-tuple-element.16) | data formatting | bytes 786432 | tf_op jit(solution)/shard_map/mul | solution.py:40
  9.7 1.9 %copy.35 = f32[1,1,128,768]{2,3,1,0:T(8,128)} copy(f32[1,1,128,768]{3,2,1,0:T(8,128)} %get-tuple-element.17) | data formatting | bytes 786432 | tf_op jit(solution)/shard_map/mul | solution.py:40
  11.7 1.6 %reduce_sum.119 = f32[128,12]{0,1:T(8,128)} reduce(f32[128,12,64]{0,2,1:T(8,128)} %bitcast.113, f32[]{:T(128)} %constant.30.clone.1), dimensions={2}, to_apply=%region_2.0 | reduce | flops 96768 | bytes 399364 | tf_op jit(solution)/shard_map/reduce_sum | solution.py:40
  13.3 1.6 %reduce_sum.120 = f32[128,12]{0,1:T(8,128)} reduce(f32[128,12,64]{0,2,1:T(8,128)} %bitcast.114, f32[]{:T(128)} %constant.30.clone.1), dimensions={2}, to_apply=%region_3.0 | reduce | flops 96768 | bytes 399364 | tf_op jit(solution)/shard_map/reduce_sum | solution.py:40
  14.9 1.9 %copy.32 = f32[1,1,128,768]{2,3,1,0:T(8,128)} copy(f32[1,1,128,768]{3,2,1,0:T(8,128)} %get-tuple-element.19) | data formatting | bytes 786432 | tf_op jit(solution)/shard_map/convert_element_type | solution.py:55
  16.8 1.9 %copy.34 = f32[1,1,128,768]{2,3,1,0:T(8,128)} copy(f32[1,1,128,768]{3,2,1,0:T(8,128)} %get-tuple-element.18) | data formatting | bytes 786432 | tf_op jit(solution)/shard_map/convert_element_type | solution.py:58
  18.7 1.5 slice_reduce_fusion.1
  20.2 0.1 mul.277
  20.3 0.8 mul.284
  21.1 1.7 %copy.31 = bf16[1,1,128,768]{2,3,1,0:T(8,128)(2,1)} copy(bf16[1,1,128,768]{3,2,1,0:T(8,128)(2,1)} %get-tuple-element.20) | data formatting | bytes 393216 | tf_op jit(solution)/shard_map/slice | solution.py:61
  22.8 0.7 add_rsqrt_fusion.2
  23.5 2.6 %fusion.2 = f32[12,128,128]{1,2,0:T(8,128)} fusion(f32[128,12,64]{0,2,1:T(8,128)} %bitcast.115, f32[128,12,64]{0,2,1:T(8,128)} %bitcast.116, f32[12,64]{1,0:T(8,128)S(1)} %mul.284, f32[128,12]{0,1:T(8,128)S(1)} %get-tuple-element.23, f32[12,64]{1,0:T(8,128)S(1)} %mul.277, f32[128,12]{0,1:T(8,128)S(1)} %get-tuple-element.24), kind=kOutput, calls=%fused_computation.6 | convolution fusion | flops 25952256 | bytes 1591296 | tf_op jit(solution)/shard_map/...lhe,...mhe->...hlm/dot_general | solution.py:64
  26.1 2.4 %convolution_convert_fusion.3 = bf16[12,64,128]{2,1,0:T(8,128)(2,1)} fusion(bf16[128,12,64]{0,2,1:T(8,128)(2,1)} %bitcast.122, f32[12,128,128]{1,2,0:T(8,128)} %fusion.2), kind=kOutput, calls=%fused_computation.17 | convolution fusion | flops 25659008 | bytes 1179648 | tf_op jit(solution)/shard_map/...hlm,...mhe->...lhe/dot_general | solution.py:68
  28.5 2.4 %fusion.18 = bf16[1,1,128,768]{3,2,1,0:T(8,128)(2,1)} fusion(bf16[128,768]{0,1:T(8,128)(2,1)} %bitcast.121, bf16[768,768]{1,0:T(8,128)(2,1)} %param.10, bf16[1,1,128,768]{3,2,1,0:T(8,128)(2,1)} %param.7), kind=kOutput, calls=%fused_computation.16 | convolution fusion | flops 151289856 | bytes 1769472 | tf_op jit(solution)/shard_map/dot_general | solution.py:72
  30.9 1.7 %reshape.411 = bf16[1,64,2,1,768]{4,2,1,3,0:T(2,128)(2,1)} reshape(bf16[1,1,128,768]{3,2,1,0:T(8,128)(2,1)} %fusion.18) | data formatting | bytes 393216 | tf_op jit(solution)/shard_map/reshape | solution.py:83
  32.6 18.9 %all-to-all-start = ((bf16[1,64,2,1,768]{4,2,3,0,1:T(2,128)(2,1)}), bf16[1,64,2,1,768]{4,2,3,0,1:T(2,128)(2,1)}, u32[]{:S(2)}, u32[]{:S(2)}) async-start(bf16[1,64,2,1,768]{4,2,3,0,1:T(2,128)(2,1)} %bitcast.117), calls=%async_computation | async-start | bytes 393216 | tf_op jit(solution)/shard_map/all_to_all | solution.py:84
  51.5 0.0 copy-done.4
  51.5 0.1 mul.299
  51.6 0.8 mul.306
  52.3 10.8 %all-to-all-done = bf16[1,64,2,1,768]{4,2,3,0,1:T(2,128)(2,1)} async-done(((bf16[1,64,2,1,768]{4,2,3,0,1:T(2,128)(2,1)}), bf16[1,64,2,1,768]{4,2,3,0,1:T(2,128)(2,1)}, u32[]{:S(2)}, u32[]{:S(2)}) %all-to-all-start) | async-done | bytes 196640 | tf_op jit(solution)/shard_map/all_to_all | solution.py:84
  63.1 1.0 bitcast_reduce_fusion
  64.2 0.6 broadcast_multiply_fusion.1
  64.7 1.3 div.65
  66.0 1.1 fusion.27
  67.1 0.6 add_rsqrt_fusion.4
  67.7 1.3 rsqrt.59
  69.0 1.1 fusion.30
  70.1 2.7 %convolution_convert_fusion = bf16[128,2304]{1,0:T(8,128)(2,1)S(1)} fusion(bf16[128,768]{1,0:T(8,128)(2,1)S(1)} %fusion.30, bf16[768,2304]{1,0:T(8,128)(2,1)} %param.11), kind=kOutput, calls=%fused_computation | convolution fusion | flops 453279744 | bytes 4325376 | tf_op jit(solution)/shard_map/dot_general | solution.py:47
  72.8 1.0 slice_convert_fusion.1
  73.7 0.9 fusion.47
  74.7 2.2 %reshape.414 = f32[2,64,12,64]{3,2,1,0:T(8,128)} reshape(f32[1,1,2,64,768]{4,3,2,1,0:T(8,128)} %get-tuple-element.13) | data formatting | bytes 786432 | tf_op jit(solution)/shard_map/reshape | solution.py:55
  76.9 2.3 %mul.296 = f32[2,64,12,64]{3,2,1,0:T(8,128)} reshape(f32[1,1,2,64,768]{4,3,2,1,0:T(8,128)} %get-tuple-element.11) | data formatting | bytes 786432 | tf_op jit(solution)/shard_map/mul | solution.py:40
  79.2 2.2 %reduce_sum.124 = f32[2,64,12]{2,1,0:T(8,128)} reduce(f32[2,64,12,64]{3,2,1,0:T(8,128)} %mul.296, f32[]{:T(128)} %constant.30.clone.1), dimensions={3}, to_apply=%region_7.0 | reduce | flops 96768 | bytes 399364 | tf_op jit(solution)/shard_map/reduce_sum | solution.py:40
  81.4 1.5 add_rsqrt_fusion.1
  82.8 2.3 %reshape.415 = f32[2,64,12,64]{3,2,1,0:T(8,128)} reshape(f32[1,1,2,64,768]{4,3,2,1,0:T(8,128)} %get-tuple-element.14) | data formatting | bytes 786432 | tf_op jit(solution)/shard_map/reshape | solution.py:59
  85.1 2.2 %mul.303 = f32[2,64,12,64]{3,2,1,0:T(8,128)} reshape(f32[1,1,2,64,768]{4,3,2,1,0:T(8,128)} %get-tuple-element.12) | data formatting | bytes 786432 | tf_op jit(solution)/shard_map/mul | solution.py:40
  87.3 2.2 %reduce_sum.125 = f32[2,64,12]{2,1,0:T(8,128)} reduce(f32[2,64,12,64]{3,2,1,0:T(8,128)} %mul.303, f32[]{:T(128)} %constant.30.clone.1), dimensions={3}, to_apply=%region_8.0 | reduce | flops 96768 | bytes 399364 | tf_op jit(solution)/shard_map/reduce_sum | solution.py:40
  89.5 1.5 add_rsqrt_fusion
  91.0 1.9 %copy.39 = bf16[1,1,2,64,768]{3,4,2,1,0:T(8,128)(2,1)} copy(bf16[1,1,2,64,768]{4,3,2,1,0:T(8,128)(2,1)} %get-tuple-element.15) | data formatting | bytes 393216 | tf_op jit(solution)/shard_map/slice | solution.py:61
  92.9 1.7 %multiply_convert_fusion.1 = bf16[2,64,12,64]{3,2,1,0:T(8,128)(2,1)S(1)} fusion(f32[2,64,12,64]{3,2,1,0:T(8,128)} %reshape.414, f32[12,64]{1,0:T(8,128)S(1)} %mul.299, f32[2,64,12]{2,1,0:T(8,128)} %add_rsqrt_fusion.1), kind=kLoop, calls=%fused_computation.22 | loop fusion | flops 294912 | bytes 599040 | tf_op jit(solution)/shard_map/convert_element_type | solution.py:41
  94.6 0.3 multiply_convert_fusion
  94.9 1.2 fusion.1
  96.1 2.5 %convolution_convert_fusion.2 = bf16[2,12,64,64]{3,2,1,0:T(8,128)(2,1)} fusion(bf16[2,64,12,64]{1,3,2,0:T(8,128)(2,1)} %bitcast.119, f32[2,12,64,64]{2,3,1,0:T(8,128)} %fusion.1), kind=kOutput, calls=%fused_computation.7 | convolution fusion | flops 12879423 | bytes 786432 | tf_op jit(solution)/shard_map/...hlm,...mhe->...lhe/dot_general | solution.py:68
  98.7 1.8 %convert_reduce_fusion.2 = (f32[768]{0:T(1024)S(1)}, bf16[2,64,768]{2,1,0:T(8,128)(2,1)S(1)}) fusion(bf16[2,64,768]{1,2,0:T(8,128)(2,1)} %bitcast.120, bf16[768,768]{1,0:T(8,128)(2,1)} %param.12, bf16[1,64,2,1,768]{4,2,3,0,1:T(2,128)(2,1)} %all-to-all-done), kind=kOutput, calls=%fused_computation.44 | convolution fusion | flops 151682304 | bytes 1772544 | tf_op jit(solution)/shard_map/dot_general | solution.py:72
  100.5 0.3 copy.44
  100.9 19.5 %all_to_all.32 = bf16[1,1,4,64,768]{4,2,1,0,3:T(4,128)(2,1)S(1)} all-to-all(bf16[1,1,4,64,768]{4,2,1,0,3:T(4,128)(2,1)S(1)} %copy.44), channel_id=1, replica_groups=mesh['seq'=64,'clip'=16] {'seq'}, dimensions={3} | all-to-all | bytes 786432 | tf_op jit(solution)/shard_map/all_to_all | solution.py:97
  120.3 0.7 copy-done.2
  121.1 0.3 convert_reduce_fusion.1
  121.4 0.6 multiply_reduce_fusion
  122.7 0.6 broadcast_in_dim.8
  123.3 14.9 %all-to-all-start.2 = ((f32[16,1,768]{2,1,0:T(1,128)}), f32[16,1,768]{2,1,0:T(1,128)}, u32[]{:S(2)}, u32[]{:S(2)}) async-start(f32[16,1,768]{2,1,0:T(1,128)} %broadcast_in_dim.8), calls=%async_computation.2 | async-start | bytes 98304 | tf_op jit(solution)/shard_map/all_to_all | solution.py:14
  138.2 0.6 mul.315
  138.8 1.8 %slice.62 = bf16[1,64,2,1,768]{4,2,1,3,0:T(2,128)(2,1)} slice(bf16[1,64,4,1,768]{4,2,1,3,0:T(4,128)(2,1)} %bitcast.112), slice={[0:1], [0:64], [0:2], [0:1], [0:768]} | slice | bytes 393216 | tf_op jit(solution)/shard_map/slice | solution.py:98
  140.6 1.7 %reshape.416 = bf16[1,1,128,768]{3,2,1,0:T(8,128)(2,1)} reshape(bf16[1,64,2,1,768]{4,2,1,3,0:T(2,128)(2,1)} %slice.62) | data formatting | bytes 393216 | tf_op jit(solution)/shard_map/reshape | solution.py:98
  142.3 7.7 %all-to-all-done.2 = f32[16,1,768]{2,1,0:T(1,128)} async-done(((f32[16,1,768]{2,1,0:T(1,128)}), f32[16,1,768]{2,1,0:T(1,128)}, u32[]{:S(2)}, u32[]{:S(2)}) %all-to-all-start.2) | async-done | bytes 49184 | tf_op jit(solution)/shard_map/all_to_all | solution.py:14
  150.0 1.5 fusion.20
  (14 shorter events, 0.1 us)
Async XLA Ops:
  0.6 3.7 %copy-start = (bf16[768,2304]{1,0:T(8,128)(2,1)S(1)}, bf16[768,2304]{1,0:T(8,128)(2,1)}, u32[]{:S(2)}) copy-start(bf16[768,2304]{1,0:T(8,128)(2,1)} %param.9) | copy-start | bytes 10616836
  28.5 23.0 %copy-start.4 = (f32[768]{0:T(1024)S(1)}, f32[768]{0:T(1024)}, u32[]{:S(2)}) copy-start(f32[768]{0:T(1024)} %get-tuple-element.3) | copy-start | bytes 9220
  32.6 30.6 %all-to-all-start = ((bf16[1,64,2,1,768]{4,2,3,0,1:T(2,128)(2,1)}), bf16[1,64,2,1,768]{4,2,3,0,1:T(2,128)(2,1)}, u32[]{:S(2)}, u32[]{:S(2)}) async-start(bf16[1,64,2,1,768]{4,2,3,0,1:T(2,128)(2,1)} %bitcast.117), calls=%async_computation | async-start | bytes 393216 | tf_op jit(solution)/shard_map/all_to_all | solution.py:84
  92.9 1.7 %copy-start.1 = (f32[2,64,12,64]{3,2,1,0:T(8,128)S(1)}, f32[2,64,12,64]{3,2,1,0:T(8,128)}, u32[]{:S(2)}) copy-start(f32[2,64,12,64]{3,2,1,0:T(8,128)} %reshape.415) | copy-start | bytes 1179652
  92.9 1.7 %copy-start.3 = (f32[2,64,12]{2,1,0:T(8,128)S(1)}, f32[2,64,12]{2,1,0:T(8,128)}, u32[]{:S(2)}) copy-start(f32[2,64,12]{2,1,0:T(8,128)} %add_rsqrt_fusion) | copy-start | bytes 18436
  120.3 0.7 copy-start.2
  123.3 26.7 %all-to-all-start.2 = ((f32[16,1,768]{2,1,0:T(1,128)}), f32[16,1,768]{2,1,0:T(1,128)}, u32[]{:S(2)}, u32[]{:S(2)}) async-start(f32[16,1,768]{2,1,0:T(1,128)} %broadcast_in_dim.8), calls=%async_computation.2 | async-start | bytes 98304 | tf_op jit(solution)/shard_map/all_to_all | solution.py:14

commit v3 on v2

--- a/solution.py
+++ b/solution.py
@@ -1,8 +1,11 @@
+import functools
 import math
 
 import jax
 import jax.numpy as jnp
 from jax import lax
+from jax.experimental import pallas as pl
+from jax.experimental.pallas import tpu as pltpu
 from jax.sharding import PartitionSpec as P
 
 D = 768
@@ -73,27 +76,104 @@
     return branch.reshape(leading + (channels,))
 
 
+def attention_kernel(groups, temporal, x_ref, ln_ref, w_ref, wo_ref, gq_ref, gk_ref, out_ref, qkv_ref, ctx_ref):
+    rows, channels = x_ref.shape
+    pairs = channels // 128
+    span = rows // groups
+    widened = x_ref[...].astype(jnp.float32)
+    average = jnp.mean(widened, axis=-1, keepdims=True)
+    centred = widened - average
+    spread = jnp.mean(centred * centred, axis=-1, keepdims=True)
+    normed = (centred * lax.rsqrt(spread + 1e-05) * ln_ref[...]).astype(jnp.bfloat16)
+    qkv_ref[...] = jnp.dot(normed, w_ref[...], preferred_element_type=jnp.float32).astype(jnp.bfloat16)
+    lane = lax.broadcasted_iota(jnp.int32, (1, 128), 1)
+    first = lane < 64
+
+    def pair_norm(values, gains):
+        squares = values * values
+        even = jnp.sum(jnp.where(first, squares, 0.0), axis=-1, keepdims=True) * (1.0 / 64)
+        odd = jnp.sum(jnp.where(first, 0.0, squares), axis=-1, keepdims=True) * (1.0 / 64)
+        inverse = jnp.where(first, lax.rsqrt(even + 1e-06), lax.rsqrt(odd + 1e-06))
+        return (values * inverse * gains).astype(jnp.bfloat16)
+
+    for p in range(pairs):
+        cols = slice(p * 128, (p + 1) * 128)
+        queries = qkv_ref[:, p * 128 : (p + 1) * 128].astype(jnp.float32)
+        keys = qkv_ref[:, channels + p * 128 : channels + (p + 1) * 128].astype(jnp.float32)
+        values = qkv_ref[:, 2 * channels + p * 128 : 2 * channels + (p + 1) * 128]
+        query_n = pair_norm(queries, gq_ref[:, cols])
+        key_n = pair_norm(keys, gk_ref[:, cols])
+        zero = jnp.zeros_like(query_n)
+        heads = (jnp.where(first, query_n, zero), jnp.where(first, zero, query_n))
+        for g in range(groups):
+            part = slice(g * span, (g + 1) * span)
+            outs = []
+            for query_h in heads:
+                scores = lax.dot_general(
+                    query_h[part], key_n[part], (((1,), (1,)), ((), ())),
+                    preferred_element_type=jnp.float32,
+                ) * 0.125
+                raised = jnp.exp(scores)
+                weights = (raised / jnp.sum(raised, axis=-1, keepdims=True)).astype(jnp.bfloat16)
+                outs.append(jnp.dot(weights, values[part], preferred_element_type=jnp.float32))
+            ctx_ref[part, cols] = jnp.where(first, outs[0], outs[1]).astype(jnp.bfloat16)
+    branch = jnp.dot(ctx_ref[...], wo_ref[...], preferred_element_type=jnp.float32)
+    if temporal:
+        branch = branch.astype(jnp.bfloat16).astype(jnp.float32)
+    result = (x_ref[...].astype(jnp.float32) + branch).astype(jnp.bfloat16)
+    out_ref[:rows, :] = result
+    if temporal:
+        partial = jnp.sum(result.astype(jnp.float32), axis=0, keepdims=True)
+        high = partial.astype(jnp.bfloat16)
+        low = (partial - high.astype(jnp.float32)).astype(jnp.bfloat16)
+        out_ref[rows : rows + span, :] = jnp.broadcast_to(high, (span, channels))
+        out_ref[rows + span :, :] = jnp.broadcast_to(low, (span, channels))
+
+
+def attention_block(tokens, ln_gain, proj, out_weight, gain_query, gain_key, groups, temporal):
+    rows, channels = tokens.shape
+    span = rows // groups
+    out_rows = rows + 2 * span if temporal else rows
+    flops = 2 * rows * channels * 3 * channels + 2 * rows * channels * channels + 8 * rows * span * channels
+    return pl.pallas_call(
+        functools.partial(attention_kernel, groups, temporal),
+        out_shape=jax.ShapeDtypeStruct((out_rows, channels), jnp.bfloat16),
+        scratch_shapes=[
+            pltpu.VMEM((rows, 3 * channels), jnp.bfloat16),
+            pltpu.VMEM((rows, channels), jnp.bfloat16),
+        ],
+        cost_estimate=pl.CostEstimate(
+            flops=flops,
+            transcendentals=2 * rows * span * HEADS,
+            bytes_accessed=2 * (4 * channels * channels + 2 * rows * channels + 2 * span * channels),
+        ),
+    )(
+        tokens,
+        ln_gain.reshape(1, channels),
+        proj,
+        out_weight,
+        gain_query.reshape(1, channels),
+        gain_key.reshape(1, channels),
+    )
+
+
 def on_device(frames_in, norm_gains, space_proj, space_out, time_proj, time_out, qk_gains):
     clips_here, frames_here, patch_count, channels = frames_in.shape
     groups = lax.axis_size("seq")
     per_group = patch_count // groups
-    spatial_in = layer_norm(frames_in, norm_gains[0])
-    branch = attention(project(spatial_in, space_proj), space_out, qk_gains[0], qk_gains[1])
-    middle = (frames_in.astype(jnp.float32) + branch).astype(jnp.bfloat16)
+    tokens = frames_in.reshape(clips_here * frames_here * patch_count, channels)
+    middle = attention_block(
+        tokens, norm_gains[0], space_proj, space_out, qk_gains[0], qk_gains[1],
+        clips_here * frames_here, False,
+    )
     outgoing = middle.reshape(clips_here, groups, per_group, frames_here, channels)
     arrived = lax.all_to_all(outgoing, "seq", split_axis=1, concat_axis=3, tiled=True)
-    temporal_in = layer_norm(arrived, norm_gains[1])
-    branch_t = attention(
-        project(temporal_in, time_proj), time_out, qk_gains[2], qk_gains[3]
-    ).astype(jnp.bfloat16)
-    block_t = (arrived.astype(jnp.float32) + branch_t.astype(jnp.float32)).astype(jnp.bfloat16)
-    partial = jnp.sum(block_t.astype(jnp.float32), axis=(2, 3), keepdims=True)
-    high = partial.astype(jnp.bfloat16)
-    low = (partial - high.astype(jnp.float32)).astype(jnp.bfloat16)
-    spread_shape = (clips_here, 1, 1, block_t.shape[3], channels)
-    payload = jnp.concatenate(
-        [block_t, jnp.broadcast_to(high, spread_shape), jnp.broadcast_to(low, spread_shape)], axis=2
-    )
+    arrived = arrived.reshape(-1, channels)
+    payload = attention_block(
+        arrived, norm_gains[1], time_proj, time_out, qk_gains[2], qk_gains[3],
+        clips_here * per_group, True,
+    )
+    payload = payload.reshape(clips_here, 1, per_group + 2, -1, channels)
     returned = lax.all_to_all(payload, "seq", split_axis=3, concat_axis=1, tiled=True)
     block_out = returned[:, :, :per_group].reshape(clips_here, frames_here, patch_count, channels)
     sums = returned[:, :, per_group:].astype(jnp.float32)

time: 153 us -> 101 us (0.66)
  blocking collectives: 19.5 us -> 48.5 us
  local copies, waits for them, and re-layouts: 34.9 us -> 6.6 us
  other arithmetic: 24.6 us -> 0.89 us
  matrix products: 18.6 us -> 0.67 us
  starting transfers between devices: 33.8 us -> 16.1 us
  Pallas kernels: 0 us -> 16.1 us
  waiting for transfers between devices: 18.5 us -> 10.2 us
    all_to_all x0 -> x1, blocking collectives: none -> 29.1 us  [on_device(): lax.all_to_all(outgoing, 'seq', split_axis=1, concat_axis=3, tiled=True)]
    all_to_all x1 -> x0, starting transfers between devices: 18.9 us -> none  [on_device(): lax.all_to_all(outgoing, 'seq', split_axis=1, concat_axis=3, tiled=True)]
    dot_general x8 -> x0, matrix products: 17.2 us -> none  [the longest x2 4.9 us: attention(): jnp.einsum('...hlm,...mhe->...lhe', attn_weights, value_part, preferred_e...]
    pallas_call x0 -> x2, Pallas kernels: none -> 16.1 us  [attention_block(): pl.pallas_call(functools.partial(attention_kernel, groups, temporal), out...]
    reduce_sum x8 -> x0, other arithmetic: 11.9 us -> none  [the longest x4 7.62 us: head_norm(): jnp.mean(values * values, axis=-1, keepdims=True) + 1e-06]
    all_to_all x1 -> x0, waiting for transfers between devices: 10.8 us -> none  [on_device(): lax.all_to_all(outgoing, 'seq', split_axis=1, concat_axis=3, tiled=True)]
    mul x8 -> x0, local copies, waits for them, and re-layouts: 9.98 us -> none  [the longest x4 8.34 us: head_norm(): values * values]
    slice x4 -> x1, local copies, waits for them, and re-layouts: 6.55 us -> 1.48 us  [on_device(): qk_gains[3]]
  transfers between devices with their start and end apart: 2 -> 1, of which waited for: 2 -> 1; matrix products, arithmetic and copies ran while one was open for 3% -> 1% of each run, Pallas kernels for 0% -> 0%
where the time goes in v3:
time: 101 us; the launch traced here: 100 us
  blocking collectives  48.5 us (48%)
  Pallas kernels  16.1 us (16%)
  starting transfers between devices  16.1 us (16%)
  waiting for transfers between devices  10.2 us (10%)
  local copies, waits for them, and re-layouts  6.6 us (7%)
  between operations  1.37 us (1%)
    all_to_all x1, blocking collectives, on_device(): lax.all_to_all(outgoing, 'seq', split_axis=1, concat_axis=3, tiled=True)  29.1 us
    all_to_all x1, blocking collectives, on_device(): lax.all_to_all(payload, 'seq', split_axis=3, concat_axis=1, tiled=True)  19.5 us
    all_to_all x1, starting transfers between devices, from_everyone(): return lax.all_to_all(copies, axis, split_axis=0, concat_axis=0, tiled=True)  16.1 us
    pallas_call x2, Pallas kernels, attention_block(): pl.pallas_call(functools.partial(attention_kernel, groups, temporal), out...  16.1 us
    all_to_all x1, waiting for transfers between devices, from_everyone(): return lax.all_to_all(copies, axis, split_axis=0, concat_axis=0, tiled=True)  10.2 us
  transfers between devices with their start and end apart: 1, of which 1 were waited for; matrix products, arithmetic and copies ran while one was open for 1% of the time, Pallas kernels for 0%

profile of v3, /device:TPU:1, one launch (start us, length us, event | category | flops | bytes accessed | tf_op | source)
XLA Modules:
  0.0 100.4 jit_solution(15819331903666883564)
XLA Ops:
  0.6 1.5 %fusion.4 = (f32[1,768]{1,0:T(1,128)}, f32[1,768]{1,0:T(1,128)}, f32[1,768]{1,0:T(1,128)}, f32[1,768]{1,0:T(1,128)}, f32[1,768]{1,0:T(1,128)}, /*index=5*/f32[1,768]{1,0:T(1,128)}) fusion(f32[4,768]{1,0:T(4,128)} %param.13, f32[2,768]{1,0:T(2,128)} %param.8), kind=kLoop, calls=%fused_computation.8 | loop fusion | bytes 36864 | tf_op jit(solution)/shard_map/slice | solution.py:173
  2.1 6.7 %shard_map.94 = bf16[128,768]{1,0:T(8,128)(2,1)} custom-call(bf16[128,768]{1,0:T(8,128)(2,1)} %bitcast.32, f32[1,768]{1,0:T(1,128)} %get-tuple-element.9.ln_ref, bf16[768,2304]{1,0:T(8,128)(2,1)} %w_ref.2, bf16[768,768]{1,0:T(8,128)(2,1)} %wo_ref.2, f32[1,768]{1,0:T(1,128)} %get-tuple-element.5.gq_ref, f32[1,768]{1,0:T(1,128)} %get-tuple-element.4.gk_ref), custom_call_target="tpu_custom_call" | custom-call | flops 704643072 | bytes 5505024 | tf_op jit(solution)/shard_map/pallas_call | solution.py:138
  8.8 1.0 reshape.65
  9.8 29.1 %all_to_all.38 = bf16[1,64,2,1,768]{4,2,3,0,1:T(2,128)(2,1)S(1)} all-to-all(bf16[1,64,2,1,768]{4,2,3,0,1:T(2,128)(2,1)S(1)} %bitcast.30), channel_id=1, replica_groups=mesh['seq'=64,'clip'=16] {'seq'}, dimensions={1} | all-to-all | bytes 393216 | tf_op jit(solution)/shard_map/all_to_all | solution.py:170
  38.8 0.7 copy.13
  39.5 9.4 %shard_map.95 = bf16[256,768]{1,0:T(8,128)(2,1)} custom-call(bf16[128,768]{1,0:T(8,128)(2,1)} %bitcast.29, f32[1,768]{1,0:T(1,128)} %get-tuple-element.10.ln_ref, bf16[768,2304]{1,0:T(8,128)(2,1)} %w_ref.3, bf16[768,768]{1,0:T(8,128)(2,1)} %wo_ref.3, f32[1,768]{1,0:T(1,128)} %get-tuple-element.6.gq_ref, f32[1,768]{1,0:T(1,128)} %get-tuple-element.3.gk_ref), custom_call_target="tpu_custom_call" | custom-call | flops 654311424 | bytes 5308416 | tf_op jit(solution)/shard_map/pallas_call | solution.py:138
  48.9 1.3 %copy.14 = bf16[1,1,4,64,768]{4,2,1,0,3:T(4,128)(2,1)S(1)} copy(bf16[1,1,4,64,768]{4,3,2,1,0:T(8,128)(2,1)} %bitcast.28) | data formatting | bytes 786432 | tf_op jit(solution)/shard_map/reshape | solution.py:176
  50.2 19.5 %all_to_all.39 = bf16[1,1,4,64,768]{4,2,1,0,3:T(4,128)(2,1)S(1)} all-to-all(bf16[1,1,4,64,768]{4,2,1,0,3:T(4,128)(2,1)S(1)} %copy.14), channel_id=1, replica_groups=mesh['seq'=64,'clip'=16] {'seq'}, dimensions={3} | all-to-all | bytes 786432 | tf_op jit(solution)/shard_map/all_to_all | solution.py:177
  69.7 0.3 convert_reduce_fusion
  70.0 0.6 multiply_reduce_fusion
  71.3 0.6 broadcast_in_dim.4
  72.0 16.1 %all-to-all-start.2 = ((f32[16,1,768]{2,1,0:T(1,128)}), f32[16,1,768]{2,1,0:T(1,128)S(1)}, u32[]{:S(2)}, u32[]{:S(2)}) async-start(f32[16,1,768]{2,1,0:T(1,128)} %broadcast_in_dim.4), calls=%async_computation.2 | async-start | bytes 98304 | tf_op jit(solution)/shard_map/all_to_all | solution.py:17
  88.1 0.1 slice.32
  88.2 0.6 mul.37
  88.8 0.8 reshape.68
  89.5 10.2 %all-to-all-done.2 = f32[16,1,768]{2,1,0:T(1,128)S(1)} async-done(((f32[16,1,768]{2,1,0:T(1,128)}), f32[16,1,768]{2,1,0:T(1,128)S(1)}, u32[]{:S(2)}, u32[]{:S(2)}) %all-to-all-start.2) | async-done | bytes 49184 | tf_op jit(solution)/shard_map/all_to_all | solution.py:17
  99.7 0.7 fusion.1
  (2 shorter events, 0.0 us)
Async XLA Ops:
  72.0 27.8 %all-to-all-start.2 = ((f32[16,1,768]{2,1,0:T(1,128)}), f32[16,1,768]{2,1,0:T(1,128)S(1)}, u32[]{:S(2)}, u32[]{:S(2)}) async-start(f32[16,1,768]{2,1,0:T(1,128)} %broadcast_in_dim.4), calls=%async_computation.2 | async-start | bytes 98304 | tf_op jit(solution)/shard_map/all_to_all | solution.py:17

commit v4 on v3

--- a/solution.py
+++ b/solution.py
@@ -76,15 +76,22 @@
     return branch.reshape(leading + (channels,))
 
 
-def attention_kernel(groups, temporal, x_ref, ln_ref, w_ref, wo_ref, gq_ref, gk_ref, out_ref, qkv_ref, ctx_ref):
-    rows, channels = x_ref.shape
+def attention_kernel(groups, temporal, rows_of, x_ref, ln_ref, w_ref, wo_ref, qk_ref, out_ref, qkv_ref, ctx_ref):
+    channels = w_ref.shape[0]
+    ln_row, q_row, k_row = rows_of
+    pieces = x_ref.shape[1] // channels
+    tokens = jnp.concatenate(
+        [x_ref[:, i * channels : (i + 1) * channels] for i in range(pieces)], axis=0
+    )
+    rows = tokens.shape[0]
     pairs = channels // 128
     span = rows // groups
-    widened = x_ref[...].astype(jnp.float32)
+    widened = tokens.astype(jnp.float32)
     average = jnp.mean(widened, axis=-1, keepdims=True)
     centred = widened - average
     spread = jnp.mean(centred * centred, axis=-1, keepdims=True)
-    normed = (centred * lax.rsqrt(spread + 1e-05) * ln_ref[...]).astype(jnp.bfloat16)
+    gain = ln_ref[ln_row : ln_row + 1, :]
+    normed = (centred * lax.rsqrt(spread + 1e-05) * gain).astype(jnp.bfloat16)
     qkv_ref[...] = jnp.dot(normed, w_ref[...], preferred_element_type=jnp.float32).astype(jnp.bfloat16)
     lane = lax.broadcasted_iota(jnp.int32, (1, 128), 1)
     first = lane < 64
@@ -101,8 +108,8 @@
         queries = qkv_ref[:, p * 128 : (p + 1) * 128].astype(jnp.float32)
         keys = qkv_ref[:, channels + p * 128 : channels + (p + 1) * 128].astype(jnp.float32)
         values = qkv_ref[:, 2 * channels + p * 128 : 2 * channels + (p + 1) * 128]
-        query_n = pair_norm(queries, gq_ref[:, cols])
-        key_n = pair_norm(keys, gk_ref[:, cols])
+        query_n = pair_norm(queries, qk_ref[q_row : q_row + 1, cols])
+        key_n = pair_norm(keys, qk_ref[k_row : k_row + 1, cols])
         zero = jnp.zeros_like(query_n)
         heads = (jnp.where(first, query_n, zero), jnp.where(first, zero, query_n))
         for g in range(groups):
@@ -120,24 +127,28 @@
     branch = jnp.dot(ctx_ref[...], wo_ref[...], preferred_element_type=jnp.float32)
     if temporal:
         branch = branch.astype(jnp.bfloat16).astype(jnp.float32)
-    result = (x_ref[...].astype(jnp.float32) + branch).astype(jnp.bfloat16)
-    out_ref[:rows, :] = result
+    result = (widened + branch).astype(jnp.bfloat16)
+    sends = out_ref.shape[0]
+    blocks = rows // sends
+    for i in range(blocks):
+        out_ref[:, i * channels : (i + 1) * channels] = result[i * sends : (i + 1) * sends]
     if temporal:
         partial = jnp.sum(result.astype(jnp.float32), axis=0, keepdims=True)
         high = partial.astype(jnp.bfloat16)
         low = (partial - high.astype(jnp.float32)).astype(jnp.bfloat16)
-        out_ref[rows : rows + span, :] = jnp.broadcast_to(high, (span, channels))
-        out_ref[rows + span :, :] = jnp.broadcast_to(low, (span, channels))
-
-
-def attention_block(tokens, ln_gain, proj, out_weight, gain_query, gain_key, groups, temporal):
-    rows, channels = tokens.shape
+        out_ref[:, blocks * channels : (blocks + 1) * channels] = jnp.broadcast_to(high, (sends, channels))
+        out_ref[:, (blocks + 1) * channels :] = jnp.broadcast_to(low, (sends, channels))
+
+
+def attention_block(tokens, norm_gains, proj, out_weight, qk_gains, rows_of, groups, temporal, sends):
+    channels = proj.shape[0]
+    rows = tokens.size // channels
     span = rows // groups
-    out_rows = rows + 2 * span if temporal else rows
+    lanes = (rows // sends + (2 if temporal else 0)) * channels
     flops = 2 * rows * channels * 3 * channels + 2 * rows * channels * channels + 8 * rows * span * channels
     return pl.pallas_call(
-        functools.partial(attention_kernel, groups, temporal),
-        out_shape=jax.ShapeDtypeStruct((out_rows, channels), jnp.bfloat16),
+        functools.partial(attention_kernel, groups, temporal, rows_of),
+        out_shape=jax.ShapeDtypeStruct((sends, lanes), jnp.bfloat16),
         scratch_shapes=[
             pltpu.VMEM((rows, 3 * channels), jnp.bfloat16),
             pltpu.VMEM((rows, channels), jnp.bfloat16),
@@ -145,16 +156,9 @@
         cost_estimate=pl.CostEstimate(
             flops=flops,
             transcendentals=2 * rows * span * HEADS,
-            bytes_accessed=2 * (4 * channels * channels + 2 * rows * channels + 2 * span * channels),
+            bytes_accessed=2 * (4 * channels * channels + 2 * rows * channels + sends * lanes),
         ),
-    )(
-        tokens,
-        ln_gain.reshape(1, channels),
-        proj,
-        out_weight,
-        gain_query.reshape(1, channels),
-        gain_key.reshape(1, channels),
-    )
+    )(tokens, norm_gains, proj, out_weight, qk_gains)
 
 
 def on_device(frames_in, norm_gains, space_proj, space_out, time_proj, time_out, qk_gains):
@@ -162,22 +166,21 @@
     groups = lax.axis_size("seq")
     per_group = patch_count // groups
     tokens = frames_in.reshape(clips_here * frames_here * patch_count, channels)
-    middle = attention_block(
-        tokens, norm_gains[0], space_proj, space_out, qk_gains[0], qk_gains[1],
-        clips_here * frames_here, False,
-    )
-    outgoing = middle.reshape(clips_here, groups, per_group, frames_here, channels)
-    arrived = lax.all_to_all(outgoing, "seq", split_axis=1, concat_axis=3, tiled=True)
-    arrived = arrived.reshape(-1, channels)
+    outgoing = attention_block(
+        tokens, norm_gains, space_proj, space_out, qk_gains, (0, 0, 1),
+        clips_here * frames_here, False, groups,
+    )
+    arrived = lax.all_to_all(outgoing, "seq", split_axis=0, concat_axis=0, tiled=True)
     payload = attention_block(
-        arrived, norm_gains[1], time_proj, time_out, qk_gains[2], qk_gains[3],
-        clips_here * per_group, True,
-    )
-    payload = payload.reshape(clips_here, 1, per_group + 2, -1, channels)
-    returned = lax.all_to_all(payload, "seq", split_axis=3, concat_axis=1, tiled=True)
-    block_out = returned[:, :, :per_group].reshape(clips_here, frames_here, patch_count, channels)
-    sums = returned[:, :, per_group:].astype(jnp.float32)
-    pooled_total = jnp.sum(sums, axis=(1, 2, 3))
+        arrived, norm_gains, time_proj, time_out, qk_gains, (1, 2, 3),
+        clips_here * per_group, True, arrived.shape[0],
+    )
+    returned = lax.all_to_all(payload, "seq", split_axis=0, concat_axis=0, tiled=True)
+    block_out = jnp.concatenate(
+        [returned[:, i * channels : (i + 1) * channels] for i in range(per_group)], axis=0
+    ).reshape(clips_here, frames_here, patch_count, channels)
+    sums = returned[:, per_group * channels :].astype(jnp.float32).reshape(-1, 2, channels)
+    pooled_total = jnp.sum(sums, axis=(0, 1)).reshape(clips_here, channels)
     pooled = pooled_total / (frames_here * patch_count * groups)
     clip_embed = pooled * lax.rsqrt(jnp.mean(pooled * pooled, axis=-1, keepdims=True) + 1e-06)
     all_embeds = collect(clip_embed, "clip", 0)

time: 101 us -> 102 us (level)
  other arithmetic: 0.89 us -> 4.86 us
  local copies, waits for them, and re-layouts: 6.6 us -> 3.39 us
    all_to_all x0 -> x2, other arithmetic: none -> 3.51 us  [the longest x1 1.86 us: on_device(): lax.all_to_all(payload, 'seq', split_axis=0, concat_axis=0, tiled=True)]
    reshape x3 -> x0, local copies, waits for them, and re-layouts: 3.05 us -> none  [the longest x1 1.3 us: on_device(): payload = payload.reshape(clips_here, 1, per_group + 2, -1, channels)]
    unnamed x0 -> x6, local copies, waits for them, and re-layouts: none -> 1.63 us
    slice x2 -> x1, local copies, waits for them, and re-layouts: 1.61 us -> 0.02 us  [on_device(): returned[:, i * channels:(i + 1) * channels]]
where the time goes in v4:
time: 102 us
  blocking collectives  48.5 us (48%)
  Pallas kernels  16.1 us (16%)
  starting transfers between devices  16.1 us (16%)
  waiting for transfers between devices  11 us (11%)
  other arithmetic  4.86 us (5%)
  local copies, waits for them, and re-layouts  3.39 us (3%)
  between operations  1.41 us (1%)
    all_to_all x1, blocking collectives, on_device(): lax.all_to_all(outgoing, 'seq', split_axis=0, concat_axis=0, tiled=True)  29.1 us
    all_to_all x1, blocking collectives, on_device(): lax.all_to_all(payload, 'seq', split_axis=0, concat_axis=0, tiled=True)  19.5 us
    pallas_call x2, Pallas kernels, attention_block(): pl.pallas_call(functools.partial(attention_kernel, groups, temporal, rows...  16.1 us
    all_to_all x1, starting transfers between devices, from_everyone(): return lax.all_to_all(copies, axis, split_axis=0, concat_axis=0, tiled=True)  16.1 us
    all_to_all x1, waiting for transfers between devices, from_everyone(): return lax.all_to_all(copies, axis, split_axis=0, concat_axis=0, tiled=True)  11 us
  transfers between devices with their start and end apart: 1, of which 1 were waited for; matrix products, arithmetic and copies ran while one was open for 1% of the time, Pallas kernels for 0%

profile of v4, /device:TPU:1, one launch (start us, length us, event | category | flops | bytes accessed | tf_op | source)
XLA Modules:
  0.0 102.0 jit_solution(10085967650380201726)
XLA Ops:
  0.6 6.7 %shard_map.94 = bf16[64,1536]{1,0:T(8,128)(2,1)} custom-call(bf16[128,768]{1,0:T(8,128)(2,1)} %bitcast.28, f32[2,768]{1,0:T(2,128)} %ln_ref.3, bf16[768,2304]{1,0:T(8,128)(2,1)} %w_ref.2, bf16[768,768]{1,0:T(8,128)(2,1)} %wo_ref.2, f32[4,768]{1,0:T(4,128)} %qk_ref.3), custom_call_target="tpu_custom_call" | custom-call | flops 704643072 | bytes 5308416 | tf_op jit(solution)/shard_map/pallas_call | solution.py:149
  7.3 0.5 broadcast.27
  7.8 1.6 %reduce.3 = bf16[64,1536]{1,0:T(8,128)(2,1)S(1)} reduce(bf16[64,1,1536]{2,0,1:T(8,128)(2,1)} %bitcast.26, bf16[]{:T(256)} %broadcast.27), dimensions={1}, to_apply=%copy.14.reduce_sub_computation | reduce | bytes 393218 | tf_op jit(solution)/shard_map/all_to_all | solution.py:173
  9.5 0.1 reshape.58
  9.5 29.1 %all_to_all.28 = bf16[64,2,768]{2,1,0:T(2,128)(2,1)S(1)} all-to-all(bf16[64,2,768]{2,1,0:T(2,128)(2,1)S(1)} %reshape.58), channel_id=1, replica_groups=mesh['seq'=64,'clip'=16] {'seq'}, dimensions={0} | all-to-all | bytes 393216 | tf_op jit(solution)/shard_map/all_to_all | solution.py:173
  38.6 0.1 reshape.59
  38.7 0.7 copy.26
  39.4 9.4 %shard_map.95 = bf16[64,3072]{1,0:T(8,128)(2,1)} custom-call(bf16[64,1536]{1,0:T(8,128)(2,1)} %bitcast.27, f32[2,768]{1,0:T(2,128)} %ln_ref.3, bf16[768,2304]{1,0:T(8,128)(2,1)} %w_ref.3, bf16[768,768]{1,0:T(8,128)(2,1)} %wo_ref.3, f32[4,768]{1,0:T(4,128)} %qk_ref.3), custom_call_target="tpu_custom_call" | custom-call | flops 654311424 | bytes 5505024 | tf_op jit(solution)/shard_map/pallas_call | solution.py:149
  48.9 1.9 %reduce.4 = bf16[64,3072]{1,0:T(8,128)(2,1)S(1)} reduce(bf16[64,1,3072]{2,0,1:T(8,128)(2,1)} %bitcast.23, bf16[]{:T(256)} %broadcast.27), dimensions={1}, to_apply=%copy.15.reduce_sub_computation | reduce | bytes 786434 | tf_op jit(solution)/shard_map/all_to_all | solution.py:178
  50.7 0.3 reshape.60
  51.0 19.5 %all_to_all.29 = bf16[64,2,1536]{2,1,0:T(2,128)(2,1)S(1)} all-to-all(bf16[64,2,1536]{2,1,0:T(2,128)(2,1)S(1)} %reshape.60), channel_id=1, replica_groups=mesh['seq'=64,'clip'=16] {'seq'}, dimensions={0} | all-to-all | bytes 786432 | tf_op jit(solution)/shard_map/all_to_all | solution.py:178
  70.5 0.3 reshape.61
  70.8 0.1 copy.25
  71.1 0.6 multiply_reduce_fusion
  72.4 0.6 mul.33
  73.0 0.6 broadcast_in_dim.4
  73.6 16.1 %all-to-all-start.2 = ((f32[16,1,768]{2,1,0:T(1,128)}), f32[16,1,768]{2,1,0:T(1,128)S(1)}, u32[]{:S(2)}, u32[]{:S(2)}) async-start(f32[16,1,768]{2,1,0:T(1,128)} %broadcast_in_dim.4), calls=%async_computation.2 | async-start | bytes 98304 | tf_op jit(solution)/shard_map/all_to_all | solution.py:17
  89.7 0.7 maximum_bitcast_fusion
  90.4 11.0 %all-to-all-done.2 = f32[16,1,768]{2,1,0:T(1,128)S(1)} async-done(((f32[16,1,768]{2,1,0:T(1,128)}), f32[16,1,768]{2,1,0:T(1,128)S(1)}, u32[]{:S(2)}, u32[]{:S(2)}) %all-to-all-start.2) | async-done | bytes 49184 | tf_op jit(solution)/shard_map/all_to_all | solution.py:17
  101.3 0.7 fusion.1
  (6 shorter events, 0.1 us)
Async XLA Ops:
  73.6 27.7 %all-to-all-start.2 = ((f32[16,1,768]{2,1,0:T(1,128)}), f32[16,1,768]{2,1,0:T(1,128)S(1)}, u32[]{:S(2)}, u32[]{:S(2)}) async-start(f32[16,1,768]{2,1,0:T(1,128)} %broadcast_in_dim.4), calls=%async_computation.2 | async-start | bytes 98304 | tf_op jit(solution)/shard_map/all_to_all | solution.py:17

commit v5 on v3

--- a/solution.py
+++ b/solution.py
@@ -76,8 +76,22 @@
     return branch.reshape(leading + (channels,))
 
 
-def attention_kernel(groups, temporal, x_ref, ln_ref, w_ref, wo_ref, gq_ref, gk_ref, out_ref, qkv_ref, ctx_ref):
+def attention_kernel(
+    groups, temporal, x_ref, ln_ref, w_hbm, wo_hbm, gq_ref, gk_ref, out_ref, qkv_ref, ctx_ref,
+    w_ref, wo_ref, sems,
+):
     rows, channels = x_ref.shape
+    loads = [
+        pltpu.make_async_copy(
+            w_hbm.at[:, j * channels : (j + 1) * channels],
+            w_ref.at[:, j * channels : (j + 1) * channels],
+            sems.at[j],
+        )
+        for j in range(3)
+    ]
+    loads.append(pltpu.make_async_copy(wo_hbm, wo_ref, sems.at[3]))
+    for load in loads:
+        load.start()
     pairs = channels // 128
     span = rows // groups
     widened = x_ref[...].astype(jnp.float32)
@@ -85,7 +99,12 @@
     centred = widened - average
     spread = jnp.mean(centred * centred, axis=-1, keepdims=True)
     normed = (centred * lax.rsqrt(spread + 1e-05) * ln_ref[...]).astype(jnp.bfloat16)
-    qkv_ref[...] = jnp.dot(normed, w_ref[...], preferred_element_type=jnp.float32).astype(jnp.bfloat16)
+    for j in range(3):
+        loads[j].wait()
+        block = slice(j * channels, (j + 1) * channels)
+        qkv_ref[:, block] = jnp.dot(
+            normed, w_ref[:, block], preferred_element_type=jnp.float32
+        ).astype(jnp.bfloat16)
     lane = lax.broadcasted_iota(jnp.int32, (1, 128), 1)
     first = lane < 64
 
@@ -117,6 +136,7 @@
                 weights = (raised / jnp.sum(raised, axis=-1, keepdims=True)).astype(jnp.bfloat16)
                 outs.append(jnp.dot(weights, values[part], preferred_element_type=jnp.float32))
             ctx_ref[part, cols] = jnp.where(first, outs[0], outs[1]).astype(jnp.bfloat16)
+    loads[3].wait()
     branch = jnp.dot(ctx_ref[...], wo_ref[...], preferred_element_type=jnp.float32)
     if temporal:
         branch = branch.astype(jnp.bfloat16).astype(jnp.float32)
@@ -138,9 +158,20 @@
     return pl.pallas_call(
         functools.partial(attention_kernel, groups, temporal),
         out_shape=jax.ShapeDtypeStruct((out_rows, channels), jnp.bfloat16),
+        in_specs=[
+            pl.BlockSpec(memory_space=pltpu.VMEM),
+            pl.BlockSpec(memory_space=pltpu.VMEM),
+            pl.BlockSpec(memory_space=pl.ANY),
+            pl.BlockSpec(memory_space=pl.ANY),
+            pl.BlockSpec(memory_space=pltpu.VMEM),
+            pl.BlockSpec(memory_space=pltpu.VMEM),
+        ],
         scratch_shapes=[
             pltpu.VMEM((rows, 3 * channels), jnp.bfloat16),
             pltpu.VMEM((rows, channels), jnp.bfloat16),
+            pltpu.VMEM((channels, 3 * channels), jnp.bfloat16),
+            pltpu.VMEM((channels, channels), jnp.bfloat16),
+            pltpu.SemaphoreType.DMA((4,)),
         ],
         cost_estimate=pl.CostEstimate(
             flops=flops,

time: 101 us -> 101 us (level)
  no operation moved by 1% of the time
where the time goes in v5:
time: 101 us
  blocking collectives  48.5 us (48%)
  Pallas kernels  16.4 us (16%)
  starting transfers between devices  16.1 us (16%)
  waiting for transfers between devices  10.2 us (10%)
  local copies, waits for them, and re-layouts  6.6 us (7%)
  between operations  1.38 us (1%)
    all_to_all x1, blocking collectives, on_device(): lax.all_to_all(outgoing, 'seq', split_axis=1, concat_axis=3, tiled=True)  29.1 us
    all_to_all x1, blocking collectives, on_device(): lax.all_to_all(payload, 'seq', split_axis=3, concat_axis=1, tiled=True)  19.5 us
    pallas_call x2, Pallas kernels, attention_block(): pl.pallas_call(functools.partial(attention_kernel, groups, temporal), out...  16.4 us
    all_to_all x1, starting transfers between devices, from_everyone(): return lax.all_to_all(copies, axis, split_axis=0, concat_axis=0, tiled=True)  16.1 us
    all_to_all x1, waiting for transfers between devices, from_everyone(): return lax.all_to_all(copies, axis, split_axis=0, concat_axis=0, tiled=True)  10.2 us
  transfers between devices with their start and end apart: 1, of which 1 were waited for; matrix products, arithmetic and copies ran while one was open for 1% of the time, Pallas kernels for 0%

profile of v5, /device:TPU:1, one launch (start us, length us, event | category | flops | bytes accessed | tf_op | source)
XLA Modules:
  0.0 100.7 jit_solution(5871564676351248166)
XLA Ops:
  0.6 1.5 %fusion.4 = (f32[1,768]{1,0:T(1,128)}, f32[1,768]{1,0:T(1,128)}, f32[1,768]{1,0:T(1,128)}, f32[1,768]{1,0:T(1,128)}, f32[1,768]{1,0:T(1,128)}, /*index=5*/f32[1,768]{1,0:T(1,128)}) fusion(f32[4,768]{1,0:T(4,128)} %param.13, f32[2,768]{1,0:T(2,128)} %param.8), kind=kLoop, calls=%fused_computation.8 | loop fusion | bytes 36864 | tf_op jit(solution)/shard_map/slice | solution.py:204
  2.1 6.8 %shard_map.94 = bf16[128,768]{1,0:T(8,128)(2,1)} custom-call(bf16[128,768]{1,0:T(8,128)(2,1)} %bitcast.32, f32[1,768]{1,0:T(1,128)} %get-tuple-element.9.ln_ref, bf16[768,2304]{1,0:T(8,128)(2,1)} %w_hbm.2, bf16[768,768]{1,0:T(8,128)(2,1)} %wo_hbm.2, f32[1,768]{1,0:T(1,128)} %get-tuple-element.5.gq_ref, f32[1,768]{1,0:T(1,128)} %get-tuple-element.4.gk_ref), custom_call_target="tpu_custom_call" | custom-call | flops 704643072 | bytes 5505024 | tf_op jit(solution)/shard_map/pallas_call | solution.py:158
  8.9 1.0 reshape.65
  9.9 29.1 %all_to_all.38 = bf16[1,64,2,1,768]{4,2,3,0,1:T(2,128)(2,1)S(1)} all-to-all(bf16[1,64,2,1,768]{4,2,3,0,1:T(2,128)(2,1)S(1)} %bitcast.30), channel_id=1, replica_groups=mesh['seq'=64,'clip'=16] {'seq'}, dimensions={1} | all-to-all | bytes 393216 | tf_op jit(solution)/shard_map/all_to_all | solution.py:201
  39.0 0.7 copy.13
  39.7 9.6 %shard_map.95 = bf16[256,768]{1,0:T(8,128)(2,1)} custom-call(bf16[128,768]{1,0:T(8,128)(2,1)} %bitcast.29, f32[1,768]{1,0:T(1,128)} %get-tuple-element.10.ln_ref, bf16[768,2304]{1,0:T(8,128)(2,1)} %w_hbm.3, bf16[768,768]{1,0:T(8,128)(2,1)} %wo_hbm.3, f32[1,768]{1,0:T(1,128)} %get-tuple-element.6.gq_ref, f32[1,768]{1,0:T(1,128)} %get-tuple-element.3.gk_ref), custom_call_target="tpu_custom_call" | custom-call | flops 654311424 | bytes 5308416 | tf_op jit(solution)/shard_map/pallas_call | solution.py:158
  49.3 1.3 %copy.14 = bf16[1,1,4,64,768]{4,2,1,0,3:T(4,128)(2,1)S(1)} copy(bf16[1,1,4,64,768]{4,3,2,1,0:T(8,128)(2,1)} %bitcast.28) | data formatting | bytes 786432 | tf_op jit(solution)/shard_map/reshape | solution.py:207
  50.6 19.5 %all_to_all.39 = bf16[1,1,4,64,768]{4,2,1,0,3:T(4,128)(2,1)S(1)} all-to-all(bf16[1,1,4,64,768]{4,2,1,0,3:T(4,128)(2,1)S(1)} %copy.14), channel_id=1, replica_groups=mesh['seq'=64,'clip'=16] {'seq'}, dimensions={3} | all-to-all | bytes 786432 | tf_op jit(solution)/shard_map/all_to_all | solution.py:208
  70.1 0.3 convert_reduce_fusion
  70.3 0.6 multiply_reduce_fusion
  71.7 0.6 broadcast_in_dim.4
  72.3 16.1 %all-to-all-start.2 = ((f32[16,1,768]{2,1,0:T(1,128)}), f32[16,1,768]{2,1,0:T(1,128)S(1)}, u32[]{:S(2)}, u32[]{:S(2)}) async-start(f32[16,1,768]{2,1,0:T(1,128)} %broadcast_in_dim.4), calls=%async_computation.2 | async-start | bytes 98304 | tf_op jit(solution)/shard_map/all_to_all | solution.py:17
  88.4 0.1 slice.32
  88.5 0.6 mul.37
  89.1 0.8 reshape.68
  89.9 10.2 %all-to-all-done.2 = f32[16,1,768]{2,1,0:T(1,128)S(1)} async-done(((f32[16,1,768]{2,1,0:T(1,128)}), f32[16,1,768]{2,1,0:T(1,128)S(1)}, u32[]{:S(2)}, u32[]{:S(2)}) %all-to-all-start.2) | async-done | bytes 49184 | tf_op jit(solution)/shard_map/all_to_all | solution.py:17
  100.0 0.7 fusion.1
  (2 shorter events, 0.0 us)
Async XLA Ops:
  72.3 27.8 %all-to-all-start.2 = ((f32[16,1,768]{2,1,0:T(1,128)}), f32[16,1,768]{2,1,0:T(1,128)S(1)}, u32[]{:S(2)}, u32[]{:S(2)}) async-start(f32[16,1,768]{2,1,0:T(1,128)} %broadcast_in_dim.4), calls=%async_computation.2 | async-start | bytes 98304 | tf_op jit(solution)/shard_map/all_to_all | solution.py:17

commit v6 on v3

--- a/solution.py
+++ b/solution.py
@@ -76,7 +76,8 @@
     return branch.reshape(leading + (channels,))
 
 
-def attention_kernel(groups, temporal, x_ref, ln_ref, w_ref, wo_ref, gq_ref, gk_ref, out_ref, qkv_ref, ctx_ref):
+def attention_kernel(groups, temporal, rows_of, x_ref, ln_ref, w_ref, wo_ref, qk_ref, out_ref, qkv_ref, ctx_ref):
+    ln_row, q_row, k_row = rows_of
     rows, channels = x_ref.shape
     pairs = channels // 128
     span = rows // groups
@@ -84,7 +85,8 @@
     average = jnp.mean(widened, axis=-1, keepdims=True)
     centred = widened - average
     spread = jnp.mean(centred * centred, axis=-1, keepdims=True)
-    normed = (centred * lax.rsqrt(spread + 1e-05) * ln_ref[...]).astype(jnp.bfloat16)
+    gain = ln_ref[ln_row : ln_row + 1, :]
+    normed = (centred * lax.rsqrt(spread + 1e-05) * gain).astype(jnp.bfloat16)
     qkv_ref[...] = jnp.dot(normed, w_ref[...], preferred_element_type=jnp.float32).astype(jnp.bfloat16)
     lane = lax.broadcasted_iota(jnp.int32, (1, 128), 1)
     first = lane < 64
@@ -101,8 +103,8 @@
         queries = qkv_ref[:, p * 128 : (p + 1) * 128].astype(jnp.float32)
         keys = qkv_ref[:, channels + p * 128 : channels + (p + 1) * 128].astype(jnp.float32)
         values = qkv_ref[:, 2 * channels + p * 128 : 2 * channels + (p + 1) * 128]
-        query_n = pair_norm(queries, gq_ref[:, cols])
-        key_n = pair_norm(keys, gk_ref[:, cols])
+        query_n = pair_norm(queries, qk_ref[q_row : q_row + 1, cols])
+        key_n = pair_norm(keys, qk_ref[k_row : k_row + 1, cols])
         zero = jnp.zeros_like(query_n)
         heads = (jnp.where(first, query_n, zero), jnp.where(first, zero, query_n))
         for g in range(groups):
@@ -130,13 +132,13 @@
         out_ref[rows + span :, :] = jnp.broadcast_to(low, (span, channels))
 
 
-def attention_block(tokens, ln_gain, proj, out_weight, gain_query, gain_key, groups, temporal):
+def attention_block(tokens, norm_gains, proj, out_weight, qk_gains, rows_of, groups, temporal):
     rows, channels = tokens.shape
     span = rows // groups
     out_rows = rows + 2 * span if temporal else rows
     flops = 2 * rows * channels * 3 * channels + 2 * rows * channels * channels + 8 * rows * span * channels
     return pl.pallas_call(
-        functools.partial(attention_kernel, groups, temporal),
+        functools.partial(attention_kernel, groups, temporal, rows_of),
         out_shape=jax.ShapeDtypeStruct((out_rows, channels), jnp.bfloat16),
         scratch_shapes=[
             pltpu.VMEM((rows, 3 * channels), jnp.bfloat16),
@@ -147,14 +149,7 @@
             transcendentals=2 * rows * span * HEADS,
             bytes_accessed=2 * (4 * channels * channels + 2 * rows * channels + 2 * span * channels),
         ),
-    )(
-        tokens,
-        ln_gain.reshape(1, channels),
-        proj,
-        out_weight,
-        gain_query.reshape(1, channels),
-        gain_key.reshape(1, channels),
-    )
+    )(tokens, norm_gains, proj, out_weight, qk_gains)
 
 
 def on_device(frames_in, norm_gains, space_proj, space_out, time_proj, time_out, qk_gains):
@@ -163,14 +158,14 @@
     per_group = patch_count // groups
     tokens = frames_in.reshape(clips_here * frames_here * patch_count, channels)
     middle = attention_block(
-        tokens, norm_gains[0], space_proj, space_out, qk_gains[0], qk_gains[1],
+        tokens, norm_gains, space_proj, space_out, qk_gains, (0, 0, 1),
         clips_here * frames_here, False,
     )
     outgoing = middle.reshape(clips_here, groups, per_group, frames_here, channels)
     arrived = lax.all_to_all(outgoing, "seq", split_axis=1, concat_axis=3, tiled=True)
     arrived = arrived.reshape(-1, channels)
     payload = attention_block(
-        arrived, norm_gains[1], time_proj, time_out, qk_gains[2], qk_gains[3],
+        arrived, norm_gains, time_proj, time_out, qk_gains, (1, 2, 3),
         clips_here * per_group, True,
     )
     payload = payload.reshape(clips_here, 1, per_group + 2, -1, channels)

time: 101 us -> 99.4 us (0.984)
  local copies, waits for them, and re-layouts: 6.6 us -> 5.12 us
    slice x1 -> x0, local copies, waits for them, and re-layouts: 1.48 us -> none  [on_device(): qk_gains[3]]
where the time goes in v6:
time: 99.4 us; the launch traced here: 99 us
  blocking collectives  48.5 us (49%)
  Pallas kernels  16.1 us (16%)
  starting transfers between devices  16.1 us (16%)
  waiting for transfers between devices  10.2 us (10%)
  local copies, waits for them, and re-layouts  5.12 us (5%)
  between operations  1.37 us (1%)
    all_to_all x1, blocking collectives, on_device(): lax.all_to_all(outgoing, 'seq', split_axis=1, concat_axis=3, tiled=True)  29.1 us
    all_to_all x1, blocking collectives, on_device(): lax.all_to_all(payload, 'seq', split_axis=3, concat_axis=1, tiled=True)  19.5 us
    pallas_call x2, Pallas kernels, attention_block(): pl.pallas_call(functools.partial(attention_kernel, groups, temporal, rows...  16.1 us
    all_to_all x1, starting transfers between devices, from_everyone(): return lax.all_to_all(copies, axis, split_axis=0, concat_axis=0, tiled=True)  16.1 us
    all_to_all x1, waiting for transfers between devices, from_everyone(): return lax.all_to_all(copies, axis, split_axis=0, concat_axis=0, tiled=True)  10.2 us
  transfers between devices with their start and end apart: 1, of which 1 were waited for; matrix products, arithmetic and copies ran while one was open for 1% of the time, Pallas kernels for 0%

profile of v6, /device:TPU:1, one launch (start us, length us, event | category | flops | bytes accessed | tf_op | source)
XLA Modules:
  0.0 99.0 jit_solution(2693156425103970816)
XLA Ops:
  0.6 6.7 %shard_map.94 = bf16[128,768]{1,0:T(8,128)(2,1)} custom-call(bf16[128,768]{1,0:T(8,128)(2,1)} %bitcast.32, f32[2,768]{1,0:T(2,128)} %ln_ref.3, bf16[768,2304]{1,0:T(8,128)(2,1)} %w_ref.2, bf16[768,768]{1,0:T(8,128)(2,1)} %wo_ref.2, f32[4,768]{1,0:T(4,128)} %qk_ref.3), custom_call_target="tpu_custom_call" | custom-call | flops 704643072 | bytes 5505024 | tf_op jit(solution)/shard_map/pallas_call | solution.py:140
  7.3 1.0 %reshape.65 = bf16[1,64,2,1,768]{4,2,1,3,0:T(2,128)(2,1)S(1)} reshape(bf16[128,768]{1,0:T(8,128)(2,1)} %shard_map.94) | data formatting | bytes 393216 | tf_op jit(solution)/shard_map/reshape | solution.py:164
  8.3 29.1 %all_to_all.38 = bf16[1,64,2,1,768]{4,2,3,0,1:T(2,128)(2,1)S(1)} all-to-all(bf16[1,64,2,1,768]{4,2,3,0,1:T(2,128)(2,1)S(1)} %bitcast.30), channel_id=1, replica_groups=mesh['seq'=64,'clip'=16] {'seq'}, dimensions={1} | all-to-all | bytes 393216 | tf_op jit(solution)/shard_map/all_to_all | solution.py:165
  37.4 0.7 copy.13
  38.1 9.4 %shard_map.95 = bf16[256,768]{1,0:T(8,128)(2,1)} custom-call(bf16[128,768]{1,0:T(8,128)(2,1)} %bitcast.29, f32[2,768]{1,0:T(2,128)} %ln_ref.3, bf16[768,2304]{1,0:T(8,128)(2,1)} %w_ref.3, bf16[768,768]{1,0:T(8,128)(2,1)} %wo_ref.3, f32[4,768]{1,0:T(4,128)} %qk_ref.3), custom_call_target="tpu_custom_call" | custom-call | flops 654311424 | bytes 5308416 | tf_op jit(solution)/shard_map/pallas_call | solution.py:140
  47.5 1.3 %copy.14 = bf16[1,1,4,64,768]{4,2,1,0,3:T(4,128)(2,1)S(1)} copy(bf16[1,1,4,64,768]{4,3,2,1,0:T(8,128)(2,1)} %bitcast.28) | data formatting | bytes 786432 | tf_op jit(solution)/shard_map/reshape | solution.py:171
  48.8 19.5 %all_to_all.39 = bf16[1,1,4,64,768]{4,2,1,0,3:T(4,128)(2,1)S(1)} all-to-all(bf16[1,1,4,64,768]{4,2,1,0,3:T(4,128)(2,1)S(1)} %copy.14), channel_id=1, replica_groups=mesh['seq'=64,'clip'=16] {'seq'}, dimensions={3} | all-to-all | bytes 786432 | tf_op jit(solution)/shard_map/all_to_all | solution.py:172
  68.3 0.3 convert_reduce_fusion
  68.6 0.6 multiply_reduce_fusion
  69.9 0.6 broadcast_in_dim.4
  70.5 16.1 %all-to-all-start.2 = ((f32[16,1,768]{2,1,0:T(1,128)}), f32[16,1,768]{2,1,0:T(1,128)S(1)}, u32[]{:S(2)}, u32[]{:S(2)}) async-start(f32[16,1,768]{2,1,0:T(1,128)} %broadcast_in_dim.4), calls=%async_computation.2 | async-start | bytes 98304 | tf_op jit(solution)/shard_map/all_to_all | solution.py:17
  86.6 0.1 slice.8
  86.8 0.6 mul.37
  87.3 0.8 reshape.68
  88.1 10.2 %all-to-all-done.2 = f32[16,1,768]{2,1,0:T(1,128)S(1)} async-done(((f32[16,1,768]{2,1,0:T(1,128)}), f32[16,1,768]{2,1,0:T(1,128)S(1)}, u32[]{:S(2)}, u32[]{:S(2)}) %all-to-all-start.2) | async-done | bytes 49184 | tf_op jit(solution)/shard_map/all_to_all | solution.py:17
  98.3 0.7 fusion.1
  (2 shorter events, 0.0 us)
Async XLA Ops:
  70.5 27.8 %all-to-all-start.2 = ((f32[16,1,768]{2,1,0:T(1,128)}), f32[16,1,768]{2,1,0:T(1,128)S(1)}, u32[]{:S(2)}, u32[]{:S(2)}) async-start(f32[16,1,768]{2,1,0:T(1,128)} %broadcast_in_dim.4), calls=%async_computation.2 | async-start | bytes 98304 | tf_op jit(solution)/shard_map/all_to_all | solution.py:17

commit v7 on v6

--- a/solution.py
+++ b/solution.py
@@ -89,6 +89,10 @@
     normed = (centred * lax.rsqrt(spread + 1e-05) * gain).astype(jnp.bfloat16)
     qkv_ref[...] = jnp.dot(normed, w_ref[...], preferred_element_type=jnp.float32).astype(jnp.bfloat16)
     lane = lax.broadcasted_iota(jnp.int32, (1, 128), 1)
+    same_group = (
+        lax.broadcasted_iota(jnp.int32, (rows, rows), 0) // span
+        == lax.broadcasted_iota(jnp.int32, (rows, rows), 1) // span
+    )
     first = lane < 64
 
     def pair_norm(values, gains):
@@ -107,18 +111,18 @@
         key_n = pair_norm(keys, qk_ref[k_row : k_row + 1, cols])
         zero = jnp.zeros_like(query_n)
         heads = (jnp.where(first, query_n, zero), jnp.where(first, zero, query_n))
-        for g in range(groups):
-            part = slice(g * span, (g + 1) * span)
-            outs = []
-            for query_h in heads:
-                scores = lax.dot_general(
-                    query_h[part], key_n[part], (((1,), (1,)), ((), ())),
-                    preferred_element_type=jnp.float32,
-                ) * 0.125
-                raised = jnp.exp(scores)
-                weights = (raised / jnp.sum(raised, axis=-1, keepdims=True)).astype(jnp.bfloat16)
-                outs.append(jnp.dot(weights, values[part], preferred_element_type=jnp.float32))
-            ctx_ref[part, cols] = jnp.where(first, outs[0], outs[1]).astype(jnp.bfloat16)
+        outs = []
+        for query_h in heads:
+            scores = lax.dot_general(
+                query_h, key_n, (((1,), (1,)), ((), ())),
+                preferred_element_type=jnp.float32,
+            ) * 0.125
+            raised = jnp.exp(scores)
+            if groups > 1:
+                raised = jnp.where(same_group, raised, 0.0)
+            weights = (raised / jnp.sum(raised, axis=-1, keepdims=True)).astype(jnp.bfloat16)
+            outs.append(jnp.dot(weights, values, preferred_element_type=jnp.float32))
+        ctx_ref[:, cols] = jnp.where(first, outs[0], outs[1]).astype(jnp.bfloat16)
     branch = jnp.dot(ctx_ref[...], wo_ref[...], preferred_element_type=jnp.float32)
     if temporal:
         branch = branch.astype(jnp.bfloat16).astype(jnp.float32)

time: 99.4 us -> 96.7 us (0.973)
  Pallas kernels: 16.1 us -> 13.4 us
    pallas_call x2, Pallas kernels: 16.1 us -> 13.4 us  [attention_block(): pl.pallas_call(functools.partial(attention_kernel, groups, temporal, rows...]
  transfers between devices with their start and end apart: 1 -> 1, of which waited for: 1 -> 1; matrix products, arithmetic and copies ran while one was open for 1% -> 2% of each run, Pallas kernels for 0% -> 0%
where the time goes in v7:
time: 96.7 us; the launch traced here: 96.3 us
  blocking collectives  48.5 us (50%)
  starting transfers between devices  16.1 us (17%)
  Pallas kernels  13.4 us (14%)
  waiting for transfers between devices  10.2 us (11%)
  local copies, waits for them, and re-layouts  5.12 us (5%)
  between operations  1.37 us (1%)
    all_to_all x1, blocking collectives, on_device(): lax.all_to_all(outgoing, 'seq', split_axis=1, concat_axis=3, tiled=True)  29.1 us
    all_to_all x1, blocking collectives, on_device(): lax.all_to_all(payload, 'seq', split_axis=3, concat_axis=1, tiled=True)  19.5 us
    all_to_all x1, starting transfers between devices, from_everyone(): return lax.all_to_all(copies, axis, split_axis=0, concat_axis=0, tiled=True)  16.1 us
    pallas_call x2, Pallas kernels, attention_block(): pl.pallas_call(functools.partial(attention_kernel, groups, temporal, rows...  13.4 us
    all_to_all x1, waiting for transfers between devices, from_everyone(): return lax.all_to_all(copies, axis, split_axis=0, concat_axis=0, tiled=True)  10.2 us
  transfers between devices with their start and end apart: 1, of which 1 were waited for; matrix products, arithmetic and copies ran while one was open for 2% of the time, Pallas kernels for 0%

profile of v7, /device:TPU:1, one launch (start us, length us, event | category | flops | bytes accessed | tf_op | source)
XLA Modules:
  0.0 96.3 jit_solution(16606328156990255965)
XLA Ops:
  0.6 6.7 %shard_map.94 = bf16[128,768]{1,0:T(8,128)(2,1)} custom-call(bf16[128,768]{1,0:T(8,128)(2,1)} %bitcast.32, f32[2,768]{1,0:T(2,128)} %ln_ref.3, bf16[768,2304]{1,0:T(8,128)(2,1)} %w_ref.2, bf16[768,768]{1,0:T(8,128)(2,1)} %wo_ref.2, f32[4,768]{1,0:T(4,128)} %qk_ref.3), custom_call_target="tpu_custom_call" | custom-call | flops 704643072 | bytes 5505024 | tf_op jit(solution)/shard_map/pallas_call | solution.py:144
  7.3 1.0 %reshape.65 = bf16[1,64,2,1,768]{4,2,1,3,0:T(2,128)(2,1)S(1)} reshape(bf16[128,768]{1,0:T(8,128)(2,1)} %shard_map.94) | data formatting | bytes 393216 | tf_op jit(solution)/shard_map/reshape | solution.py:168
  8.3 29.1 %all_to_all.38 = bf16[1,64,2,1,768]{4,2,3,0,1:T(2,128)(2,1)S(1)} all-to-all(bf16[1,64,2,1,768]{4,2,3,0,1:T(2,128)(2,1)S(1)} %bitcast.30), channel_id=1, replica_groups=mesh['seq'=64,'clip'=16] {'seq'}, dimensions={1} | all-to-all | bytes 393216 | tf_op jit(solution)/shard_map/all_to_all | solution.py:169
  37.4 0.7 copy.13
  38.1 6.7 %shard_map.95 = bf16[256,768]{1,0:T(8,128)(2,1)} custom-call(bf16[128,768]{1,0:T(8,128)(2,1)} %bitcast.29, f32[2,768]{1,0:T(2,128)} %ln_ref.3, bf16[768,2304]{1,0:T(8,128)(2,1)} %w_ref.3, bf16[768,768]{1,0:T(8,128)(2,1)} %wo_ref.3, f32[4,768]{1,0:T(4,128)} %qk_ref.3), custom_call_target="tpu_custom_call" | custom-call | flops 654311424 | bytes 5308416 | tf_op jit(solution)/shard_map/pallas_call | solution.py:144
  44.8 1.3 %copy.14 = bf16[1,1,4,64,768]{4,2,1,0,3:T(4,128)(2,1)S(1)} copy(bf16[1,1,4,64,768]{4,3,2,1,0:T(8,128)(2,1)} %bitcast.28) | data formatting | bytes 786432 | tf_op jit(solution)/shard_map/reshape | solution.py:175
  46.1 19.5 %all_to_all.39 = bf16[1,1,4,64,768]{4,2,1,0,3:T(4,128)(2,1)S(1)} all-to-all(bf16[1,1,4,64,768]{4,2,1,0,3:T(4,128)(2,1)S(1)} %copy.14), channel_id=1, replica_groups=mesh['seq'=64,'clip'=16] {'seq'}, dimensions={3} | all-to-all | bytes 786432 | tf_op jit(solution)/shard_map/all_to_all | solution.py:176
  65.6 0.3 convert_reduce_fusion
  65.9 0.6 multiply_reduce_fusion
  67.2 0.6 broadcast_in_dim.4
  67.8 16.1 %all-to-all-start.2 = ((f32[16,1,768]{2,1,0:T(1,128)}), f32[16,1,768]{2,1,0:T(1,128)S(1)}, u32[]{:S(2)}, u32[]{:S(2)}) async-start(f32[16,1,768]{2,1,0:T(1,128)} %broadcast_in_dim.4), calls=%async_computation.2 | async-start | bytes 98304 | tf_op jit(solution)/shard_map/all_to_all | solution.py:17
  83.9 0.1 slice.8
  84.1 0.6 mul.37
  84.7 0.8 reshape.68
  85.4 10.2 %all-to-all-done.2 = f32[16,1,768]{2,1,0:T(1,128)S(1)} async-done(((f32[16,1,768]{2,1,0:T(1,128)}), f32[16,1,768]{2,1,0:T(1,128)S(1)}, u32[]{:S(2)}, u32[]{:S(2)}) %all-to-all-start.2) | async-done | bytes 49184 | tf_op jit(solution)/shard_map/all_to_all | solution.py:17
  95.6 0.7 fusion.1
  (2 shorter events, 0.0 us)
Async XLA Ops:
  67.8 27.8 %all-to-all-start.2 = ((f32[16,1,768]{2,1,0:T(1,128)}), f32[16,1,768]{2,1,0:T(1,128)S(1)}, u32[]{:S(2)}, u32[]{:S(2)}) async-start(f32[16,1,768]{2,1,0:T(1,128)} %broadcast_in_dim.4), calls=%async_computation.2 | async-start | bytes 98304 | tf_op jit(solution)/shard_map/all_to_all | solution.py:17

commit v8 on v7

--- a/solution.py
+++ b/solution.py
@@ -90,8 +90,8 @@
     qkv_ref[...] = jnp.dot(normed, w_ref[...], preferred_element_type=jnp.float32).astype(jnp.bfloat16)
     lane = lax.broadcasted_iota(jnp.int32, (1, 128), 1)
     same_group = (
-        lax.broadcasted_iota(jnp.int32, (rows, rows), 0) // span
-        == lax.broadcasted_iota(jnp.int32, (rows, rows), 1) // span
+        lax.broadcasted_iota(jnp.int32, (rows, rows), 0) % groups
+        == lax.broadcasted_iota(jnp.int32, (rows, rows), 1) % groups
     )
     first = lane < 64
 
@@ -166,17 +166,24 @@
         clips_here * frames_here, False,
     )
     outgoing = middle.reshape(clips_here, groups, per_group, frames_here, channels)
-    arrived = lax.all_to_all(outgoing, "seq", split_axis=1, concat_axis=3, tiled=True)
+    arrived = lax.all_to_all(outgoing, "seq", split_axis=1, concat_axis=1, tiled=True)
     arrived = arrived.reshape(-1, channels)
     payload = attention_block(
         arrived, norm_gains, time_proj, time_out, qk_gains, (1, 2, 3),
         clips_here * per_group, True,
     )
-    payload = payload.reshape(clips_here, 1, per_group + 2, -1, channels)
-    returned = lax.all_to_all(payload, "seq", split_axis=3, concat_axis=1, tiled=True)
-    block_out = returned[:, :, :per_group].reshape(clips_here, frames_here, patch_count, channels)
-    sums = returned[:, :, per_group:].astype(jnp.float32)
-    pooled_total = jnp.sum(sums, axis=(1, 2, 3))
+    sends = payload.shape[0] // (per_group + 2)
+    payload = jnp.concatenate(
+        [
+            payload[: per_group * sends].reshape(sends, per_group, channels),
+            payload[per_group * sends :].reshape(2, sends, channels).transpose(1, 0, 2),
+        ],
+        axis=1,
+    )
+    returned = lax.all_to_all(payload, "seq", split_axis=0, concat_axis=0, tiled=True)
+    block_out = returned[:, :per_group].reshape(clips_here, frames_here, patch_count, channels)
+    sums = returned[:, per_group:].astype(jnp.float32)
+    pooled_total = jnp.sum(sums, axis=(0, 1)).reshape(clips_here, channels)
     pooled = pooled_total / (frames_here * patch_count * groups)
     clip_embed = pooled * lax.rsqrt(jnp.mean(pooled * pooled, axis=-1, keepdims=True) + 1e-06)
     all_embeds = collect(clip_embed, "clip", 0)

time: 96.7 us -> 97.2 us (level)
    slice x1 -> x2, local copies, waits for them, and re-layouts: 0.14 us -> 1.18 us  [the longest x1 1.05 us: on_device(): payload[:per_group * sends].reshape(sends, per_group, channels)]
    reshape x2 -> x4, local copies, waits for them, and re-layouts: 2.05 us -> 1.79 us  [the longest x1 0.75 us: on_device(): returned[:, :per_group]]
where the time goes in v8:
time: 97.2 us; the launch traced here: 96.8 us
  blocking collectives  48.5 us (50%)
  starting transfers between devices  16.1 us (17%)
  Pallas kernels  13.4 us (14%)
  waiting for transfers between devices  10.2 us (10%)
  local copies, waits for them, and re-layouts  5.2 us (5%)
  between operations  1.38 us (1%)
  other arithmetic  1.3 us (1%)
    all_to_all x1, blocking collectives, on_device(): lax.all_to_all(outgoing, 'seq', split_axis=1, concat_axis=1, tiled=True)  29.1 us
    all_to_all x1, blocking collectives, on_device(): lax.all_to_all(payload, 'seq', split_axis=0, concat_axis=0, tiled=True)  19.5 us
    all_to_all x1, starting transfers between devices, from_everyone(): return lax.all_to_all(copies, axis, split_axis=0, concat_axis=0, tiled=True)  16.1 us
    pallas_call x2, Pallas kernels, attention_block(): pl.pallas_call(functools.partial(attention_kernel, groups, temporal, rows...  13.4 us
    all_to_all x1, waiting for transfers between devices, from_everyone(): return lax.all_to_all(copies, axis, split_axis=0, concat_axis=0, tiled=True)  10.2 us
  transfers between devices with their start and end apart: 1, of which 1 were waited for; matrix products, arithmetic and copies ran while one was open for 2% of the time, Pallas kernels for 0%

profile of v8, /device:TPU:1, one launch (start us, length us, event | category | flops | bytes accessed | tf_op | source)
XLA Modules:
  0.0 96.8 jit_solution(4094608390843047063)
XLA Ops:
  0.6 6.7 %shard_map.94 = bf16[128,768]{1,0:T(8,128)(2,1)} custom-call(bf16[128,768]{1,0:T(8,128)(2,1)} %bitcast.23, f32[2,768]{1,0:T(2,128)} %ln_ref.3, bf16[768,2304]{1,0:T(8,128)(2,1)} %w_ref.2, bf16[768,768]{1,0:T(8,128)(2,1)} %wo_ref.2, f32[4,768]{1,0:T(4,128)} %qk_ref.3), custom_call_target="tpu_custom_call" | custom-call | flops 704643072 | bytes 5505024 | tf_op jit(solution)/shard_map/pallas_call | solution.py:144
  7.3 1.0 %reshape.60 = bf16[1,64,2,1,768]{4,2,1,3,0:T(2,128)(2,1)S(1)} reshape(bf16[128,768]{1,0:T(8,128)(2,1)} %shard_map.94) | data formatting | bytes 393216 | tf_op jit(solution)/shard_map/reshape | solution.py:168
  8.3 29.1 %all_to_all.15 = bf16[1,64,2,1,768]{4,2,3,0,1:T(2,128)(2,1)S(1)} all-to-all(bf16[1,64,2,1,768]{4,2,3,0,1:T(2,128)(2,1)S(1)} %bitcast.20), channel_id=1, replica_groups=mesh['seq'=64,'clip'=16] {'seq'}, dimensions={1} | all-to-all | bytes 393216 | tf_op jit(solution)/shard_map/all_to_all | solution.py:169
  37.4 0.8 reshape.61.x_ref
  38.1 6.8 %shard_map.95 = bf16[256,768]{1,0:T(8,128)(2,1)} custom-call(bf16[128,768]{1,0:T(8,128)(2,1)} %reshape.61.x_ref, f32[2,768]{1,0:T(2,128)} %ln_ref.3, bf16[768,2304]{1,0:T(8,128)(2,1)} %w_ref.3, bf16[768,768]{1,0:T(8,128)(2,1)} %wo_ref.3, f32[4,768]{1,0:T(4,128)} %qk_ref.3), custom_call_target="tpu_custom_call" | custom-call | flops 654311424 | bytes 5308416 | tf_op jit(solution)/shard_map/pallas_call | solution.py:144
  44.9 1.0 %fusion.4 = (bf16[128,768]{1,0:T(8,128)(2,1)S(1)}, bf16[128,768]{1,0:T(8,128)(2,1)S(1)}) fusion(bf16[256,768]{1,0:T(8,128)(2,1)} %shard_map.95), kind=kLoop, calls=%fused_computation.10 | loop fusion | bytes 786432 | tf_op jit(solution)/shard_map/slice | solution.py:178
  45.9 0.1 reshape.62
  46.0 0.2 copy.20
  46.2 0.4 pad_maximum_fusion
  46.6 19.5 %all_to_all.16 = bf16[64,4,768]{2,1,0:T(4,128)(2,1)S(1)} all-to-all(bf16[64,4,768]{2,1,0:T(4,128)(2,1)S(1)} %pad_maximum_fusion), channel_id=1, replica_groups=mesh['seq'=64,'clip'=16] {'seq'}, dimensions={0} | all-to-all | bytes 786432 | tf_op jit(solution)/shard_map/all_to_all | solution.py:183
  66.1 0.3 convert_reduce_fusion
  66.4 0.6 multiply_reduce_fusion
  67.7 0.6 broadcast_in_dim.4
  68.4 16.1 %all-to-all-start.2 = ((f32[16,1,768]{2,1,0:T(1,128)}), f32[16,1,768]{2,1,0:T(1,128)S(1)}, u32[]{:S(2)}, u32[]{:S(2)}) async-start(f32[16,1,768]{2,1,0:T(1,128)} %broadcast_in_dim.4), calls=%async_computation.2 | async-start | bytes 98304 | tf_op jit(solution)/shard_map/all_to_all | solution.py:17
  84.5 0.6 mul.33
  85.0 0.1 slice.18
  85.2 0.8 reshape.64
  85.9 10.2 %all-to-all-done.2 = f32[16,1,768]{2,1,0:T(1,128)S(1)} async-done(((f32[16,1,768]{2,1,0:T(1,128)}), f32[16,1,768]{2,1,0:T(1,128)S(1)}, u32[]{:S(2)}, u32[]{:S(2)}) %all-to-all-start.2) | async-done | bytes 49184 | tf_op jit(solution)/shard_map/all_to_all | solution.py:17
  96.1 0.7 fusion.1
  (2 shorter events, 0.0 us)
Async XLA Ops:
  68.4 27.8 %all-to-all-start.2 = ((f32[16,1,768]{2,1,0:T(1,128)}), f32[16,1,768]{2,1,0:T(1,128)S(1)}, u32[]{:S(2)}, u32[]{:S(2)}) async-start(f32[16,1,768]{2,1,0:T(1,128)} %broadcast_in_dim.4), calls=%async_computation.2 | async-start | bytes 98304 | tf_op jit(solution)/shard_map/all_to_all | solution.py:17

commit v9 on v7

--- a/solution.py
+++ b/solution.py
@@ -178,8 +178,11 @@
     sums = returned[:, :, per_group:].astype(jnp.float32)
     pooled_total = jnp.sum(sums, axis=(1, 2, 3))
     pooled = pooled_total / (frames_here * patch_count * groups)
+    all_pooled = collect(pooled, "clip", 0)
     clip_embed = pooled * lax.rsqrt(jnp.mean(pooled * pooled, axis=-1, keepdims=True) + 1e-06)
-    all_embeds = collect(clip_embed, "clip", 0)
+    all_embeds = all_pooled * lax.rsqrt(
+        jnp.mean(all_pooled * all_pooled, axis=-1, keepdims=True) + 1e-06
+    )
     similarity = (
         jnp.dot(
             clip_embed,

time: 96.7 us -> 96.9 us (level)
  no operation moved by 1% of the time
where the time goes in v9:
time: 96.9 us; the launch traced here: 96.5 us
  blocking collectives  48.5 us (50%)
  starting transfers between devices  16.1 us (17%)
  Pallas kernels  13.4 us (14%)
  waiting for transfers between devices  10.2 us (11%)
  local copies, waits for them, and re-layouts  5.12 us (5%)
  between operations  1.38 us (1%)
  other arithmetic  1.12 us (1%)
    all_to_all x1, blocking collectives, on_device(): lax.all_to_all(outgoing, 'seq', split_axis=1, concat_axis=3, tiled=True)  29.1 us
    all_to_all x1, blocking collectives, on_device(): lax.all_to_all(payload, 'seq', split_axis=3, concat_axis=1, tiled=True)  19.5 us
    all_to_all x1, starting transfers between devices, from_everyone(): return lax.all_to_all(copies, axis, split_axis=0, concat_axis=0, tiled=True)  16.1 us
    pallas_call x2, Pallas kernels, attention_block(): pl.pallas_call(functools.partial(attention_kernel, groups, temporal, rows...  13.4 us
    all_to_all x1, waiting for transfers between devices, from_everyone(): return lax.all_to_all(copies, axis, split_axis=0, concat_axis=0, tiled=True)  10.2 us
  transfers between devices with their start and end apart: 1, of which 1 were waited for; matrix products, arithmetic and copies ran while one was open for 2% of the time, Pallas kernels for 0%

profile of v9, /device:TPU:1, one launch (start us, length us, event | category | flops | bytes accessed | tf_op | source)
XLA Modules:
  0.0 96.5 jit_solution(650077603392828453)
XLA Ops:
  0.6 6.7 %shard_map.94 = bf16[128,768]{1,0:T(8,128)(2,1)} custom-call(bf16[128,768]{1,0:T(8,128)(2,1)} %bitcast.32, f32[2,768]{1,0:T(2,128)} %ln_ref.3, bf16[768,2304]{1,0:T(8,128)(2,1)} %w_ref.2, bf16[768,768]{1,0:T(8,128)(2,1)} %wo_ref.2, f32[4,768]{1,0:T(4,128)} %qk_ref.3), custom_call_target="tpu_custom_call" | custom-call | flops 704643072 | bytes 5505024 | tf_op jit(solution)/shard_map/pallas_call | solution.py:144
  7.3 1.0 %reshape.79 = bf16[1,64,2,1,768]{4,2,1,3,0:T(2,128)(2,1)S(1)} reshape(bf16[128,768]{1,0:T(8,128)(2,1)} %shard_map.94) | data formatting | bytes 393216 | tf_op jit(solution)/shard_map/reshape | solution.py:168
  8.3 29.1 %all_to_all.38 = bf16[1,64,2,1,768]{4,2,3,0,1:T(2,128)(2,1)S(1)} all-to-all(bf16[1,64,2,1,768]{4,2,3,0,1:T(2,128)(2,1)S(1)} %bitcast.30), channel_id=1, replica_groups=mesh['seq'=64,'clip'=16] {'seq'}, dimensions={1} | all-to-all | bytes 393216 | tf_op jit(solution)/shard_map/all_to_all | solution.py:169
  37.4 0.7 copy.23
  38.1 6.7 %shard_map.95 = bf16[256,768]{1,0:T(8,128)(2,1)} custom-call(bf16[128,768]{1,0:T(8,128)(2,1)} %bitcast.29, f32[2,768]{1,0:T(2,128)} %ln_ref.3, bf16[768,2304]{1,0:T(8,128)(2,1)} %w_ref.3, bf16[768,768]{1,0:T(8,128)(2,1)} %wo_ref.3, f32[4,768]{1,0:T(4,128)} %qk_ref.3), custom_call_target="tpu_custom_call" | custom-call | flops 654311424 | bytes 5308416 | tf_op jit(solution)/shard_map/pallas_call | solution.py:144
  44.8 1.3 %copy.24 = bf16[1,1,4,64,768]{4,2,1,0,3:T(4,128)(2,1)S(1)} copy(bf16[1,1,4,64,768]{4,3,2,1,0:T(8,128)(2,1)} %bitcast.28) | data formatting | bytes 786432 | tf_op jit(solution)/shard_map/reshape | solution.py:175
  46.1 19.5 %all_to_all.39 = bf16[1,1,4,64,768]{4,2,1,0,3:T(4,128)(2,1)S(1)} all-to-all(bf16[1,1,4,64,768]{4,2,1,0,3:T(4,128)(2,1)S(1)} %copy.24), channel_id=1, replica_groups=mesh['seq'=64,'clip'=16] {'seq'}, dimensions={3} | all-to-all | bytes 786432 | tf_op jit(solution)/shard_map/all_to_all | solution.py:176
  65.6 0.3 convert_reduce_fusion
  65.9 0.6 broadcast_multiply_fusion.2
  67.2 0.6 broadcast_in_dim.2
  67.8 16.1 %all-to-all-start.2 = ((f32[16,1,768]{2,1,0:T(1,128)}), f32[16,1,768]{2,1,0:T(1,128)S(1)}, u32[]{:S(2)}, u32[]{:S(2)}) async-start(f32[16,1,768]{2,1,0:T(1,128)} %broadcast_in_dim.2), calls=%async_computation.2 | async-start | bytes 98304 | tf_op jit(solution)/shard_map/all_to_all | solution.py:17
  83.9 0.1 slice.8
  84.1 0.6 mul.51
  84.7 0.8 reshape.82
  85.4 10.2 %all-to-all-done.2 = f32[16,1,768]{2,1,0:T(1,128)S(1)} async-done(((f32[16,1,768]{2,1,0:T(1,128)}), f32[16,1,768]{2,1,0:T(1,128)S(1)}, u32[]{:S(2)}, u32[]{:S(2)}) %all-to-all-start.2) | async-done | bytes 49184 | tf_op jit(solution)/shard_map/all_to_all | solution.py:17
  95.6 0.1 fusion.4
  95.7 0.1 broadcast_multiply_fusion
  95.8 0.7 fusion.1
  (3 shorter events, 0.0 us)
Async XLA Ops:
  67.8 27.8 %all-to-all-start.2 = ((f32[16,1,768]{2,1,0:T(1,128)}), f32[16,1,768]{2,1,0:T(1,128)S(1)}, u32[]{:S(2)}, u32[]{:S(2)}) async-start(f32[16,1,768]{2,1,0:T(1,128)} %broadcast_in_dim.2), calls=%async_computation.2 | async-start | bytes 98304 | tf_op jit(solution)/shard_map/all_to_all | solution.py:17
